TPU v7x, 256 devices: a whole 4x4x8 slice. The times are simulated.
256 devices in a mesh: chip: 2 (over core), row: 16 (over x, y), grp: 8 (over z).
Axes of the slice: x: 4, y: 4, z: 8, core: 2. Of those that a mesh axis runs over, the one named last changes fastest.
Arguments:
- old_velocity: float32 [2, 4096, 4096], P(None, 'row', ('chip', 'grp')), may hold values from -6 to 6
- surface_stress: float32 [2, 4096, 4096], P(None, 'row', ('chip', 'grp')), may hold values from -6 to 6
- mass_term: float32 [4096, 4096], P('row', ('chip', 'grp')), may hold values from 0.2 to 2
- ocean_drag: float32 [4096, 4096], P('row', ('chip', 'grp')), may hold values from 0.1 to 1
- strength: float32 [4096, 4096], P('row', ('chip', 'grp')), may hold values from 1 to 10
- ice_mask: int32 [4096, 4096], P('row', ('chip', 'grp')), may hold values from 0 to 1, as said below
- ocean_mask: int32 [4096, 4096], P('row', ('chip', 'grp')), may hold values 0 or 1
- ice_blocks: int32 [16, 32], P(('chip', 'grp')), may hold values from 0 to 63, as said below
Outputs:
- new_velocity: float32 [2, 4096, 4096], P(None, 'row', ('chip', 'grp'))
Inputs may be any that keep to these rules, and one draw needn't show every extreme that they name: `ice_blocks`: entry n of row c names block n % 4 (row-major over the blocks of 128 x 128 cells of a tile) of tile row n // 4 in tile column c. Each row lists 32 different blocks; the blocks of one tile stand together, tiles with more listed blocks first; all 4 blocks of the last tile row of every column are listed. The entry at place k of a row is owned by tile row k % 16 of that column, as its block number k // 16. `ice_mask`: ice lies only in cells of the blocks listed in ice_blocks.
All inputs are finite; a program needn't handle non-finite values. No bound on the sum of `ocean_mask` on one device may be relied on, other than what follows from the above.
Results may differ from a plain program's by a relative error of at most 0.00011.
Values sent between devices are 32-bit elements; how exact they have to be, the bound alone decides.
No kernel may reach another device: no remote copies, remote signals or barrier semaphores. Data moves between devices by JAX's collectives and lax.ppermute only.
A program may use at most 128 MiB of HBM per device.

v0:
```python
import jax
import jax.numpy as jnp
from jax import lax
from jax.experimental import pallas as pl
from jax.experimental.pallas import tpu as pltpu
from jax.sharding import PartitionSpec as P

BS = 128
KRYLOV = 2
CYCLES = 2
SWEEPS = 2


RELAX = 0.8
DMIN_SQ = 0.25
SHIFT = 1.0

COLS = ("chip", "grp")


def edges(array, axis, dim):
    size, length = (lax.axis_size(axis), array.shape[dim])
    up = [(i, i + 1) for i in range(size - 1)]
    down = [(j, i) for i, j in up]
    last = lax.slice_in_dim(array, length - 1, length, axis=dim)
    initial = lax.slice_in_dim(array, 0, 1, axis=dim)
    before = lax.ppermute(last, axis, up)
    after = lax.ppermute(initial, axis, down)
    return before, after


def extended(array):
    before, after = edges(array, "row", 1)
    array = jnp.concatenate([before, array, after], axis=1)
    before, after = edges(array, COLS, 2)
    return jnp.concatenate([before, array, after], axis=2)


def stencil(padded, zeta_field, diag_field):

    def pieces(field):
        center = field[..., 1:-1, 1:-1]
        second_x = field[..., 2:, 1:-1] + field[..., :-2, 1:-1] - 2.0 * center
        second_y = field[..., 1:-1, 2:] + field[..., 1:-1, :-2] - 2.0 * center
        mixed = 0.25 * (
            field[..., 2:, 2:] - field[..., 2:, :-2] - field[..., :-2, 2:] + field[..., :-2, :-2]
        )
        return (center, second_x, second_y, mixed)

    part_u = pieces(padded[..., 0, :, :])
    part_v = pieces(padded[..., 1, :, :])
    along_u = (
        diag_field * part_u[0]
        - 1.25 * zeta_field * part_u[1]
        - 0.25 * zeta_field * part_u[2]
        - zeta_field * part_v[3]
    )
    along_v = (
        diag_field * part_v[0]
        - 0.25 * zeta_field * part_v[1]
        - 1.25 * zeta_field * part_v[2]
        - zeta_field * part_u[3]
    )
    return jnp.stack([along_u, along_v], axis=-3)


def grid_to_blocks(tile_grid):
    channels, tile_rows, tile_cols = tile_grid.shape
    shaped = tile_grid.reshape(channels, tile_rows // BS, BS, tile_cols // BS, BS).transpose(
        1, 3, 0, 2, 4
    )
    return shaped.reshape(tile_rows // BS * (tile_cols // BS), channels, BS, BS)


def blocks_to_grid(blocks, tile_rows, tile_cols):
    channels = blocks.shape[1]
    shaped = blocks.reshape(tile_rows // BS, tile_cols // BS, channels, BS, BS).transpose(
        2, 0, 3, 1, 4
    )
    return shaped.reshape(channels, tile_rows, tile_cols)


def precondition(vector, zeta_blocks, diag_blocks):
    diagonal_total = (diag_blocks + 3.0 * zeta_blocks)[:, None]
    iterate = vector / diagonal_total
    for relaxation in range(SWEEPS):
        padded = jnp.pad(iterate, ((0, 0), (0, 0), (1, 1), (1, 1)))
        iterate = (
            iterate + RELAX * (vector - stencil(padded, zeta_blocks, diag_blocks)) / diagonal_total
        )
    return iterate


def least_squares(h, start_norm):
    steps_count = KRYLOV
    row_list = [[h[i][j] for j in range(steps_count)] for i in range(steps_count + 1)]
    target_vec = [start_norm] + [jnp.zeros_like(start_norm) for i in range(steps_count)]
    for j in range(steps_count):
        upper = row_list[j][j]
        lower = row_list[j + 1][j]
        radius = jnp.sqrt(upper * upper + lower * lower)
        cosine = upper / radius
        sine_part = lower / radius
        first_row = [cosine * p + sine_part * q for p, q in zip(row_list[j], row_list[j + 1])]
        second_row = [-sine_part * p + cosine * q for p, q in zip(row_list[j], row_list[j + 1])]
        row_list[j], row_list[j + 1] = (first_row, second_row)
        first_val = cosine * target_vec[j] + sine_part * target_vec[j + 1]
        second_val = -sine_part * target_vec[j] + cosine * target_vec[j + 1]
        target_vec[j], target_vec[j + 1] = (first_val, second_val)
    weights_out = [None] * steps_count
    for j in range(steps_count - 1, -1, -1):
        accum = target_vec[j]
        for i in range(j + 1, steps_count):
            accum = accum - row_list[j][i] * weights_out[i]
        weights_out[j] = accum / row_list[j][j]
    return weights_out


def krylov_coefficients(gram):
    count = len(gram)

    def dot(p, q):
        total = None
        for i in range(count):
            for j in range(count):
                term = p[i] * gram[i][j] * q[j]
                total = term if total is None else total + term
        return total

    def shift(p):
        return [SHIFT * p[0]] + [x + SHIFT * y for x, y in zip(p[:-1], p[1:])]

    def scale(p, s):
        return [x * s for x in p]

    def axpy(p, s, q):
        return [x - s * y for x, y in zip(p, q)]

    one = jnp.ones_like(gram[0][0])
    zero = jnp.zeros_like(gram[0][0])
    residual = [one] + [zero] * (count - 1)
    solution = [zero] * count
    for restart in range(CYCLES):
        start_norm = jnp.sqrt(dot(residual, residual))
        basis_list = [scale(residual, 1.0 / start_norm)]
        images_list = []
        h = [[zero] * KRYLOV for _ in range(KRYLOV + 1)]
        for arnoldi in range(KRYLOV):
            images = shift(basis_list[arnoldi])
            images_list.append(images)
            products = [dot(images, vector) for vector in basis_list]
            for i in range(arnoldi + 1):
                images = axpy(images, products[i], basis_list[i])
            new_norm = jnp.sqrt(dot(images, images))
            for i in range(arnoldi + 1):
                h[i][arnoldi] = products[i]
            h[arnoldi + 1][arnoldi] = new_norm
            if arnoldi + 1 < KRYLOV:
                basis_list.append(scale(images, 1.0 / new_norm))
        weights_out = least_squares(h, start_norm)
        for arnoldi in range(KRYLOV):
            solution = [u + weights_out[arnoldi] * b for u, b in zip(solution, basis_list[arnoldi])]
            residual = axpy(residual, weights_out[arnoldi], images_list[arnoldi])
    return solution


def gram_kernel(count, *refs):
    vectors = [refs[i][...] for i in range(count)]
    out_ref = refs[count]
    shape = out_ref.shape
    rows = lax.broadcasted_iota(jnp.int32, shape, 0)
    lanes = lax.broadcasted_iota(jnp.int32, shape, 1)
    result = jnp.zeros(shape, jnp.float32)
    index = 0
    for i in range(count):
        for j in range(i, count):
            product = vectors[i] * vectors[j]
            part = jnp.sum(jnp.sum(product, axis=0, keepdims=True), axis=1, keepdims=True)
            result = jnp.where((rows == 0) & (lanes == index), part, result)
            index += 1
    out_ref[...] = result


def local_gram(krylov):
    count = len(krylov)
    flat = [k.reshape(-1, k.shape[-1]) for k in krylov]
    return pl.pallas_call(
        lambda *refs: gram_kernel(count, *refs),
        out_shape=jax.ShapeDtypeStruct((8, 128), jnp.float32),
        in_specs=[pl.BlockSpec(memory_space=pltpu.VMEM)] * count,
        out_specs=pl.BlockSpec(memory_space=pltpu.VMEM),
    )(*flat)


def coefficients_kernel(count, total_ref, out_ref):
    shape = out_ref.shape
    pairs = [(i, j) for i in range(count) for j in range(i, count)]
    gram = [[None] * count for _ in range(count)]
    for index, (i, j) in enumerate(pairs):
        value = jnp.full(shape, total_ref[0, index], jnp.float32)
        gram[i][j] = value
        gram[j][i] = value
    update = krylov_coefficients(gram)
    rows = lax.broadcasted_iota(jnp.int32, shape, 0)
    result = jnp.zeros(shape, jnp.float32)
    for k, value in enumerate(update[: count - 1]):
        result = jnp.where(rows == k, value, result)
    out_ref[...] = result


def solve_small(total, count):
    out = pl.pallas_call(
        lambda total_ref, out_ref: coefficients_kernel(count, total_ref, out_ref),
        out_shape=jax.ShapeDtypeStruct((8, 128), jnp.float32),
        in_specs=[pl.BlockSpec(memory_space=pltpu.SMEM)],
        out_specs=pl.BlockSpec(memory_space=pltpu.VMEM),
    )(total)
    column = out[:, 0]
    return [column[k] for k in range(count - 1)]


def butterfly(values, axis):
    size = lax.axis_size(axis)
    stride = 1
    while stride < size:
        values = values + lax.ppermute(values, axis, [(i, i ^ stride) for i in range(size)])
        stride *= 2
    return values


def reduce_all(values):
    return butterfly(butterfly(butterfly(values, "chip"), "row"), "grp")


def shards(
    old_velocity, surface_stress, mass_term, ocean_drag, strength, ice_mask, ocean_mask, ice_blocks
):
    tile_rows = old_velocity.shape[1]
    tile_cols = old_velocity.shape[2]
    per_row = tile_cols // BS
    tile_blocks = tile_rows // BS * per_row

    rows_before, rows_after = edges(old_velocity, "row", 1)
    cols_before, cols_after = edges(old_velocity, COLS, 2)
    along_x = jnp.concatenate([rows_before, old_velocity, rows_after], axis=1)
    along_y = jnp.concatenate([cols_before, old_velocity, cols_after], axis=2)
    strain_xx = 0.5 * (along_x[0, 2:, :] - along_x[0, :-2, :])
    strain_yy = 0.5 * (along_y[1, :, 2:] - along_y[1, :, :-2])
    strain_xy = 0.25 * (
        along_y[0, :, 2:] - along_y[0, :, :-2] + along_x[1, 2:, :] - along_x[1, :-2, :]
    )
    deform_sq = (
        1.25 * (strain_xx * strain_xx + strain_yy * strain_yy)
        + strain_xy * strain_xy
        + 1.5 * strain_xx * strain_yy
    )
    is_ocean = ocean_mask.astype(jnp.float32)
    zeta_tile = (
        is_ocean * ice_mask.astype(jnp.float32) * strength / (2.0 * jnp.sqrt(deform_sq + DMIN_SQ))
    )
    diag_tile = is_ocean * (mass_term + ocean_drag) + (1.0 - is_ocean)

    my_row = lax.axis_index("row")
    listed = ice_blocks[0]
    wanted = my_row * tile_blocks + jnp.arange(tile_blocks, dtype=jnp.int32)
    flags = jnp.any(listed[:, None] == wanted[None, :], axis=0).astype(jnp.float32)
    live = jnp.repeat(
        jnp.repeat(flags.reshape(tile_rows // BS, per_row), BS, axis=0), BS, axis=1
    )
    rhs = live * is_ocean * (surface_stress + mass_term * old_velocity)

    zeta_blocks = grid_to_blocks(zeta_tile[None])[:, 0]
    diag_blocks = grid_to_blocks(diag_tile[None])[:, 0]

    def apply_system(vector):
        return live * stencil(extended(vector), zeta_tile, diag_tile)

    def apply_precond(vector):
        return blocks_to_grid(
            precondition(grid_to_blocks(vector), zeta_blocks, diag_blocks), tile_rows, tile_cols
        )

    krylov = [rhs]
    directions = []
    for step in range(CYCLES * KRYLOV):
        directions.append(apply_precond(krylov[-1]))
        krylov.append(apply_system(directions[-1]) - SHIFT * krylov[-1])
    total = reduce_all(local_gram(krylov))
    update = solve_small(total, len(krylov))
    solution = update[0] * directions[0]
    for i in range(1, len(directions)):
        solution = solution + update[i] * directions[i]
    return solution


def solution(mesh):
    return jax.shard_map(
        shards,
        mesh=mesh,
        in_specs=(
            P(None, "row", COLS),
            P(None, "row", COLS),
            P("row", COLS),
            P("row", COLS),
            P("row", COLS),
            P("row", COLS),
            P("row", COLS),
            P(COLS, None),
        ),
        out_specs=P(None, "row", COLS),
        check_vma=False,
    )
```

profile of v0, /device:TPU:24, one launch (start us, length us, event | category | flops | bytes accessed | tf_op | source)
XLA Modules:
  0.0 207.2 jit_solution(8713666025146670480)
XLA Ops:
  0.8 2.6 %collective-permute-start = (f32[2,1,256]{2,1,0:T(1,128)S(1)}, f32[2,1,256]{2,1,0:T(1,128)S(1)}, u32[]{:S(2)}, u32[]{:S(2)}) collective-permute-start(f32[2,1,256]{2,1,0:T(1,128)S(1)} %get-tuple-element.50), channel_id=1, source_target_pairs={{8,0},{16,8},{24,16},{32,24},{40,32},{48,40},{56,48},{64,56},{72,6... | collective-permute-start | bytes 6152 | tf_op jit(solution)/shard_map/ppermute | solution.py:28
  3.4 5.3 %collective-permute-start.1 = (f32[2,1,256]{2,1,0:T(1,128)S(1)}, f32[2,1,256]{2,1,0:T(1,128)S(1)}, u32[]{:S(2)}, u32[]{:S(2)}) collective-permute-start(f32[2,1,256]{2,1,0:T(1,128)S(1)} %get-tuple-element.51), channel_id=1, source_target_pairs={{0,8},{8,16},{16,24},{24,32},{32,40},{40,48},{48,56},{56,64},{64,7... | collective-permute-start | bytes 6152 | tf_op jit(solution)/shard_map/ppermute | solution.py:27
  8.7 1.9 fusion.305
  10.7 1.4 collective-permute-start.2
  12.1 5.3 %collective-permute-start.3 = (f32[2,256,1]{2,1,0:T(8,128)}, f32[2,256,1]{2,1,0:T(8,128)}, u32[]{:S(2)}, u32[]{:S(2)}) collective-permute-start(f32[2,256,1]{2,1,0:T(8,128)} %get-tuple-element.46), channel_id=1, source_target_pairs={{0,1},{1,2},{2,3},{3,4},{4,5},{5,6},{6,7},{7,128},{128,129},{129,1... | collective-permute-start | bytes 6152 | tf_op jit(solution)/shard_map/ppermute | solution.py:27
  20.7 1.7 constant_dynamic-update-slice_fusion.1
  22.4 2.0 subtract_add_fusion
  28.9 2.2 %collective-permute-start.4 = (f32[2,1,256]{2,1,0:T(1,128)S(1)}, f32[2,1,256]{2,1,0:T(1,128)S(1)}, u32[]{:S(2)}, u32[]{:S(2)}) collective-permute-start(f32[2,1,256]{2,1,0:T(1,128)S(1)} %get-tuple-element.39), channel_id=1, source_target_pairs={{0,8},{8,16},{16,24},{24,32},{32,40},{40,48},{48,56},{56,64},{64,7... | collective-permute-start | bytes 6152 | tf_op jit(solution)/shard_map/ppermute | solution.py:27
  31.2 3.8 %collective-permute-start.5 = (f32[2,1,256]{2,1,0:T(1,128)S(1)}, f32[2,1,256]{2,1,0:T(1,128)S(1)}, u32[]{:S(2)}, u32[]{:S(2)}) collective-permute-start(f32[2,1,256]{2,1,0:T(1,128)S(1)} %get-tuple-element.40), channel_id=1, source_target_pairs={{8,0},{16,8},{24,16},{32,24},{40,32},{48,40},{56,48},{64,56},{72,6... | collective-permute-start | bytes 6152 | tf_op jit(solution)/shard_map/ppermute | solution.py:28
  35.0 3.9 %collective-permute-done.5 = f32[2,1,256]{2,1,0:T(1,128)S(1)} collective-permute-done((f32[2,1,256]{2,1,0:T(1,128)S(1)}, f32[2,1,256]{2,1,0:T(1,128)S(1)}, u32[]{:S(2)}, u32[]{:S(2)}) %collective-permute-start.5) | collective-permute-done | bytes 2080 | tf_op jit(solution)/shard_map/ppermute | solution.py:28
  39.1 3.8 %collective-permute-start.6 = (f32[2,258,1]{2,1,0:T(8,128)S(1)}, f32[2,258,1]{2,1,0:T(8,128)S(1)}, u32[]{:S(2)}, u32[]{:S(2)}) collective-permute-start(f32[2,258,1]{2,1,0:T(8,128)S(1)} %get-tuple-element.19), channel_id=1, source_target_pairs={{0,1},{1,2},{2,3},{3,4},{4,5},{5,6},{6,7},{7,128},{128,129},{129,1... | collective-permute-start | bytes 6200 | tf_op jit(solution)/shard_map/ppermute | solution.py:27
  42.9 1.5 collective-permute-start.7
  44.4 3.8 %collective-permute-done.6 = f32[2,258,1]{2,1,0:T(8,128)S(1)} collective-permute-done((f32[2,258,1]{2,1,0:T(8,128)S(1)}, f32[2,258,1]{2,1,0:T(8,128)S(1)}, u32[]{:S(2)}, u32[]{:S(2)}) %collective-permute-start.6) | collective-permute-done | bytes 2096 | tf_op jit(solution)/shard_map/ppermute | solution.py:27
  48.2 4.7 %collective-permute-done.7 = f32[2,258,1]{2,1,0:T(8,128)S(1)} collective-permute-done((f32[2,258,1]{2,1,0:T(8,128)S(1)}, f32[2,258,1]{2,1,0:T(8,128)S(1)}, u32[]{:S(2)}, u32[]{:S(2)}) %collective-permute-start.7) | collective-permute-done | bytes 2096 | tf_op jit(solution)/shard_map/ppermute | solution.py:28
  55.5 2.1 %reshape.176 = f32[2,2,128,2,128]{4,3,2,1,0:T(2,128)} reshape(f32[2,256,256]{2,1,0:T(8,128)} %fusion.26) | data formatting | bytes 1048576 | tf_op jit(solution)/shard_map/reshape | solution.py:69
  57.6 1.1 copy.129
  62.3 1.2 copy.111
  63.5 1.5 reshape.178
  65.0 1.9 collective-permute-start.8
  66.9 3.9 %collective-permute-start.9 = (f32[2,1,256]{2,1,0:T(1,128)S(1)}, f32[2,1,256]{2,1,0:T(1,128)S(1)}, u32[]{:S(2)}, u32[]{:S(2)}) collective-permute-start(f32[2,1,256]{2,1,0:T(1,128)S(1)} %get-tuple-element.34), channel_id=1, source_target_pairs={{8,0},{16,8},{24,16},{32,24},{40,32},{48,40},{56,48},{64,56},{72,6... | collective-permute-start | bytes 6152 | tf_op jit(solution)/shard_map/ppermute | solution.py:28
  70.9 3.6 %collective-permute-done.9 = f32[2,1,256]{2,1,0:T(1,128)S(1)} collective-permute-done((f32[2,1,256]{2,1,0:T(1,128)S(1)}, f32[2,1,256]{2,1,0:T(1,128)S(1)}, u32[]{:S(2)}, u32[]{:S(2)}) %collective-permute-start.9) | collective-permute-done | bytes 2080 | tf_op jit(solution)/shard_map/ppermute | solution.py:28
  74.7 3.2 %collective-permute-start.10 = (f32[2,258,1]{2,1,0:T(8,128)S(1)}, f32[2,258,1]{2,1,0:T(8,128)S(1)}, u32[]{:S(2)}, u32[]{:S(2)}) collective-permute-start(f32[2,258,1]{2,1,0:T(8,128)S(1)} %get-tuple-element.17), channel_id=1, source_target_pairs={{0,1},{1,2},{2,3},{3,4},{4,5},{5,6},{6,7},{7,128},{128,129},{129,1... | collective-permute-start | bytes 6200 | tf_op jit(solution)/shard_map/ppermute | solution.py:27
  77.9 1.3 collective-permute-start.11
  79.2 3.7 %collective-permute-done.10 = f32[2,258,1]{2,1,0:T(8,128)S(1)} collective-permute-done((f32[2,258,1]{2,1,0:T(8,128)S(1)}, f32[2,258,1]{2,1,0:T(8,128)S(1)}, u32[]{:S(2)}, u32[]{:S(2)}) %collective-permute-start.10) | collective-permute-done | bytes 2096 | tf_op jit(solution)/shard_map/ppermute | solution.py:27
  82.9 4.5 %collective-permute-done.11 = f32[2,258,1]{2,1,0:T(8,128)S(1)} collective-permute-done((f32[2,258,1]{2,1,0:T(8,128)S(1)}, f32[2,258,1]{2,1,0:T(8,128)S(1)}, u32[]{:S(2)}, u32[]{:S(2)}) %collective-permute-start.11) | collective-permute-done | bytes 2096 | tf_op jit(solution)/shard_map/ppermute | solution.py:28
  90.7 2.1 %reshape.180 = f32[2,2,128,2,128]{4,3,2,1,0:T(2,128)} reshape(f32[2,256,256]{2,1,0:T(8,128)} %fusion.37) | data formatting | bytes 1048576 | tf_op jit(solution)/shard_map/reshape | solution.py:69
  92.8 1.1 copy.130
  97.5 1.2 copy.119
  98.8 1.5 reshape.182
  100.2 2.1 %collective-permute-start.12 = (f32[2,1,256]{2,1,0:T(1,128)S(1)}, f32[2,1,256]{2,1,0:T(1,128)S(1)}, u32[]{:S(2)}, u32[]{:S(2)}) collective-permute-start(f32[2,1,256]{2,1,0:T(1,128)S(1)} %get-tuple-element.27), channel_id=1, source_target_pairs={{0,8},{8,16},{16,24},{24,32},{32,40},{40,48},{48,56},{56,64},{64,7... | collective-permute-start | bytes 6152 | tf_op jit(solution)/shard_map/ppermute | solution.py:27
  102.4 3.9 %collective-permute-start.13 = (f32[2,1,256]{2,1,0:T(1,128)S(1)}, f32[2,1,256]{2,1,0:T(1,128)S(1)}, u32[]{:S(2)}, u32[]{:S(2)}) collective-permute-start(f32[2,1,256]{2,1,0:T(1,128)S(1)} %get-tuple-element.28), channel_id=1, source_target_pairs={{8,0},{16,8},{24,16},{32,24},{40,32},{48,40},{56,48},{64,56},{72,6... | collective-permute-start | bytes 6152 | tf_op jit(solution)/shard_map/ppermute | solution.py:28
  106.3 3.6 %collective-permute-done.13 = f32[2,1,256]{2,1,0:T(1,128)S(1)} collective-permute-done((f32[2,1,256]{2,1,0:T(1,128)S(1)}, f32[2,1,256]{2,1,0:T(1,128)S(1)}, u32[]{:S(2)}, u32[]{:S(2)}) %collective-permute-start.13) | collective-permute-done | bytes 2080 | tf_op jit(solution)/shard_map/ppermute | solution.py:28
  110.1 5.1 %collective-permute-start.14 = (f32[2,258,1]{2,1,0:T(8,128)S(1)}, f32[2,258,1]{2,1,0:T(8,128)S(1)}, u32[]{:S(2)}, u32[]{:S(2)}) collective-permute-start(f32[2,258,1]{2,1,0:T(8,128)S(1)} %get-tuple-element.15), channel_id=1, source_target_pairs={{0,1},{1,2},{2,3},{3,4},{4,5},{5,6},{6,7},{7,128},{128,129},{129,1... | collective-permute-start | bytes 6200 | tf_op jit(solution)/shard_map/ppermute | solution.py:27
  115.3 1.3 collective-permute-start.15
  116.6 2.6 %collective-permute-done.14 = f32[2,258,1]{2,1,0:T(8,128)S(1)} collective-permute-done((f32[2,258,1]{2,1,0:T(8,128)S(1)}, f32[2,258,1]{2,1,0:T(8,128)S(1)}, u32[]{:S(2)}, u32[]{:S(2)}) %collective-permute-start.14) | collective-permute-done | bytes 2096 | tf_op jit(solution)/shard_map/ppermute | solution.py:27
  119.2 4.4 %collective-permute-done.15 = f32[2,258,1]{2,1,0:T(8,128)S(1)} collective-permute-done((f32[2,258,1]{2,1,0:T(8,128)S(1)}, f32[2,258,1]{2,1,0:T(8,128)S(1)}, u32[]{:S(2)}, u32[]{:S(2)}) %collective-permute-start.15) | collective-permute-done | bytes 2096 | tf_op jit(solution)/shard_map/ppermute | solution.py:28
  127.0 2.1 %reshape.184 = f32[2,2,128,2,128]{4,3,2,1,0:T(2,128)} reshape(f32[2,256,256]{2,1,0:T(8,128)} %fusion.48) | data formatting | bytes 1048576 | tf_op jit(solution)/shard_map/reshape | solution.py:69
  129.1 1.1 copy.131
  133.9 1.2 copy.127
  135.1 1.5 reshape.186
  136.5 1.9 collective-permute-start.16
  138.5 3.9 %collective-permute-start.17 = (f32[2,1,256]{2,1,0:T(1,128)S(1)}, f32[2,1,256]{2,1,0:T(1,128)S(1)}, u32[]{:S(2)}, u32[]{:S(2)}) collective-permute-start(f32[2,1,256]{2,1,0:T(1,128)S(1)} %get-tuple-element.22), channel_id=1, source_target_pairs={{8,0},{16,8},{24,16},{32,24},{40,32},{48,40},{56,48},{64,56},{72,6... | collective-permute-start | bytes 6152 | tf_op jit(solution)/shard_map/ppermute | solution.py:28
  142.4 3.6 %collective-permute-done.17 = f32[2,1,256]{2,1,0:T(1,128)S(1)} collective-permute-done((f32[2,1,256]{2,1,0:T(1,128)S(1)}, f32[2,1,256]{2,1,0:T(1,128)S(1)}, u32[]{:S(2)}, u32[]{:S(2)}) %collective-permute-start.17) | collective-permute-done | bytes 2080 | tf_op jit(solution)/shard_map/ppermute | solution.py:28
  146.2 3.9 %collective-permute-start.18 = (f32[2,258,1]{2,1,0:T(8,128)S(1)}, f32[2,258,1]{2,1,0:T(8,128)S(1)}, u32[]{:S(2)}, u32[]{:S(2)}) collective-permute-start(f32[2,258,1]{2,1,0:T(8,128)S(1)} %get-tuple-element.13), channel_id=1, source_target_pairs={{0,1},{1,2},{2,3},{3,4},{4,5},{5,6},{6,7},{7,128},{128,129},{129,1... | collective-permute-start | bytes 6200 | tf_op jit(solution)/shard_map/ppermute | solution.py:27
  150.2 1.3 collective-permute-start.19
  151.5 2.6 %collective-permute-done.18 = f32[2,258,1]{2,1,0:T(8,128)S(1)} collective-permute-done((f32[2,258,1]{2,1,0:T(8,128)S(1)}, f32[2,258,1]{2,1,0:T(8,128)S(1)}, u32[]{:S(2)}, u32[]{:S(2)}) %collective-permute-start.18) | collective-permute-done | bytes 2096 | tf_op jit(solution)/shard_map/ppermute | solution.py:27
  154.1 4.4 %collective-permute-done.19 = f32[2,258,1]{2,1,0:T(8,128)S(1)} collective-permute-done((f32[2,258,1]{2,1,0:T(8,128)S(1)}, f32[2,258,1]{2,1,0:T(8,128)S(1)}, u32[]{:S(2)}, u32[]{:S(2)}) %collective-permute-start.19) | collective-permute-done | bytes 2096 | tf_op jit(solution)/shard_map/ppermute | solution.py:28
  161.9 3.0 %shard_map.82 = f32[8,128]{1,0:T(8,128)} custom-call(f32[512,256]{1,0:T(8,128)} %bitcast.319, f32[512,256]{1,0:T(8,128)} %bitcast.324, f32[512,256]{1,0:T(8,128)} %bitcast.333, f32[512,256]{1,0:T(8,128)} %bitcast.334, f32[512,256]{1,0:T(8,128)} %bitcast.355), custom_call_target="tpu_custom_call" | custom-call | tf_op jit(solution)/shard_map/pallas_call | solution.py:187
  164.8 1.4 collective-permute-done.20
  166.9 3.6 %collective-permute-done.21 = f32[8,128]{1,0:T(8,128)S(1)} collective-permute-done((f32[8,128]{1,0:T(8,128)S(1)}, f32[8,128]{1,0:T(8,128)S(1)}, u32[]{:S(2)}, u32[]{:S(2)}) %collective-permute-start.21) | collective-permute-done | bytes 4128 | tf_op jit(solution)/shard_map/ppermute | solution.py:226
  170.5 5.1 %collective-permute-done.22 = f32[8,128]{1,0:T(8,128)S(1)} collective-permute-done((f32[8,128]{1,0:T(8,128)S(1)}, f32[8,128]{1,0:T(8,128)S(1)}, u32[]{:S(2)}, u32[]{:S(2)}) %collective-permute-start.22) | collective-permute-done | bytes 4128 | tf_op jit(solution)/shard_map/ppermute | solution.py:226
  175.6 1.5 collective-permute-start.23
  177.1 2.1 %collective-permute-done.23 = f32[8,128]{1,0:T(8,128)S(1)} collective-permute-done((f32[8,128]{1,0:T(8,128)S(1)}, f32[8,128]{1,0:T(8,128)S(1)}, u32[]{:S(2)}, u32[]{:S(2)}) %collective-permute-start.23) | collective-permute-done | bytes 4128 | tf_op jit(solution)/shard_map/ppermute | solution.py:226
  179.2 3.0 %collective-permute-start.24 = (f32[8,128]{1,0:T(8,128)S(1)}, f32[8,128]{1,0:T(8,128)S(1)}, u32[]{:S(2)}, u32[]{:S(2)}) collective-permute-start(f32[8,128]{1,0:T(8,128)S(1)} %add.460), channel_id=1, source_target_pairs={{0,64},{8,72},{16,80},{24,88},{32,96},{40,104},{48,112},{56,120},{... | collective-permute-start | bytes 12296 | tf_op jit(solution)/shard_map/ppermute | solution.py:226
  182.3 2.1 %collective-permute-done.24 = f32[8,128]{1,0:T(8,128)S(1)} collective-permute-done((f32[8,128]{1,0:T(8,128)S(1)}, f32[8,128]{1,0:T(8,128)S(1)}, u32[]{:S(2)}, u32[]{:S(2)}) %collective-permute-start.24) | collective-permute-done | bytes 4128 | tf_op jit(solution)/shard_map/ppermute | solution.py:226
  184.4 1.2 collective-permute-start.25
  185.6 2.4 %collective-permute-done.25 = f32[8,128]{1,0:T(8,128)S(1)} collective-permute-done((f32[8,128]{1,0:T(8,128)S(1)}, f32[8,128]{1,0:T(8,128)S(1)}, u32[]{:S(2)}, u32[]{:S(2)}) %collective-permute-start.25) | collective-permute-done | bytes 4128 | tf_op jit(solution)/shard_map/ppermute | solution.py:226
  188.0 1.9 collective-permute-start.26
  189.8 2.6 %collective-permute-done.26 = f32[8,128]{1,0:T(8,128)S(1)} collective-permute-done((f32[8,128]{1,0:T(8,128)S(1)}, f32[8,128]{1,0:T(8,128)S(1)}, u32[]{:S(2)}, u32[]{:S(2)}) %collective-permute-start.26) | collective-permute-done | bytes 4128 | tf_op jit(solution)/shard_map/ppermute | solution.py:226
  192.5 1.5 collective-permute-start.27
  194.0 6.0 %collective-permute-done.27 = f32[8,128]{1,0:T(8,128)S(1)} collective-permute-done((f32[8,128]{1,0:T(8,128)S(1)}, f32[8,128]{1,0:T(8,128)S(1)}, u32[]{:S(2)}, u32[]{:S(2)}) %collective-permute-start.27) | collective-permute-done | bytes 4128 | tf_op jit(solution)/shard_map/ppermute | solution.py:226
  200.6 1.7 shard_map.83
  202.3 1.4 fusion.307
  203.8 3.4 %multiply_add_fusion = f32[2,256,256]{2,1,0:T(8,128)} fusion(f32[2,256,256]{2,1,0:T(8,128)S(1)} %reshape.186, f32[2,256,256]{2,1,0:T(8,128)S(1)} %reshape.182, f32[2,256,256]{2,1,0:T(8,128)S(1)} %reshape.178, f32[2,256,256]{2,1,0:T(8,128)S(1)} %reshape.174, f32[]{:T(128)} %bitcast.104, f32[]{:T(128)} %bitcast.103, f32[]{:T(128)} %bitcast.102, f32[]{:T(128)} %bitcast.101), kind=kLoop, calls=%fused_computation.104 | loop fusion | flops 917504 | bytes 2621456 | tf_op jit(solution)/shard_map/add | solution.py:292
  (177 shorter events, 33.5 us)
Async XLA Ops:
  0.0 17.4 %copy-start.33 = (s32[1,32]{1,0:T(1,128)S(1)}, s32[1,32]{1,0:T(1,128)}, u32[]{:S(2)}) copy-start(s32[1,32]{1,0:T(1,128)} %param.15) | copy-start | bytes 388
  0.0 18.7 %copy-start.31 = (s32[256,256]{1,0:T(8,128)S(1)}, s32[256,256]{1,0:T(8,128)}, u32[]{:S(2)}) copy-start(s32[256,256]{1,0:T(8,128)} %param.14) | copy-start | bytes 786436
  0.8 21.6 %collective-permute-start = (f32[2,1,256]{2,1,0:T(1,128)S(1)}, f32[2,1,256]{2,1,0:T(1,128)S(1)}, u32[]{:S(2)}, u32[]{:S(2)}) collective-permute-start(f32[2,1,256]{2,1,0:T(1,128)S(1)} %get-tuple-element.50), channel_id=1, source_target_pairs={{8,0},{16,8},{24,16},{32,24},{40,32},{48,40},{56,48},{64,56},{72,6... | collective-permute-start | bytes 6152 | tf_op jit(solution)/shard_map/ppermute | solution.py:28
  3.4 19.0 %collective-permute-start.1 = (f32[2,1,256]{2,1,0:T(1,128)S(1)}, f32[2,1,256]{2,1,0:T(1,128)S(1)}, u32[]{:S(2)}, u32[]{:S(2)}) collective-permute-start(f32[2,1,256]{2,1,0:T(1,128)S(1)} %get-tuple-element.51), channel_id=1, source_target_pairs={{0,8},{8,16},{16,24},{24,32},{32,40},{40,48},{48,56},{56,64},{64,7... | collective-permute-start | bytes 6152 | tf_op jit(solution)/shard_map/ppermute | solution.py:27
  10.7 8.1 %copy-start.14 = (f32[2,256,256]{2,1,0:T(8,128)S(1)}, f32[2,256,256]{2,1,0:T(8,128)}, u32[]{:S(2)}) copy-start(f32[2,256,256]{2,1,0:T(8,128)} %param.8) | copy-start | bytes 1572868
  10.7 8.1 %copy-start.30 = (f32[256,256]{1,0:T(8,128)S(1)}, f32[256,256]{1,0:T(8,128)}, u32[]{:S(2)}) copy-start(f32[256,256]{1,0:T(8,128)} %param.10) | copy-start | bytes 786436
  10.7 8.1 %copy-start.32 = (f32[2,256,256]{2,1,0:T(8,128)S(1)}, f32[2,256,256]{2,1,0:T(8,128)}, u32[]{:S(2)}) copy-start(f32[2,256,256]{2,1,0:T(8,128)} %param.9) | copy-start | bytes 1572868
  10.7 10.0 %collective-permute-start.2 = (f32[2,256,1]{2,1,0:T(8,128)}, f32[2,256,1]{2,1,0:T(8,128)}, u32[]{:S(2)}, u32[]{:S(2)}) collective-permute-start(f32[2,256,1]{2,1,0:T(8,128)} %get-tuple-element.45), channel_id=1, source_target_pairs={{1,0},{2,1},{3,2},{4,3},{5,4},{6,5},{7,6},{128,7},{129,128},{130,1... | collective-permute-start | bytes 6152 | tf_op jit(solution)/shard_map/ppermute | solution.py:28
  12.1 10.3 %collective-permute-start.3 = (f32[2,256,1]{2,1,0:T(8,128)}, f32[2,256,1]{2,1,0:T(8,128)}, u32[]{:S(2)}, u32[]{:S(2)}) collective-permute-start(f32[2,256,1]{2,1,0:T(8,128)} %get-tuple-element.46), channel_id=1, source_target_pairs={{0,1},{1,2},{2,3},{3,4},{4,5},{5,6},{6,7},{7,128},{128,129},{129,1... | collective-permute-start | bytes 6152 | tf_op jit(solution)/shard_map/ppermute | solution.py:27
  18.0 0.7 copy-start.24
  19.7 140.3 %copy-start = (f32[2,256,256]{2,1,0:T(8,128)}, f32[2,256,256]{2,1,0:T(8,128)S(1)}, u32[]{:S(2)}) copy-start(f32[2,256,256]{2,1,0:T(8,128)S(1)} %get-tuple-element.49) | copy-start | bytes 1572868
  27.9 68.9 %copy-start.1 = (f32[2,2,128,128]{3,2,1,0:T(8,128)}, f32[2,2,128,128]{3,2,1,0:T(8,128)S(1)}, u32[]{:S(2)}) copy-start(f32[2,2,128,128]{3,2,1,0:T(8,128)S(1)} %copy.94) | copy-start | bytes 786436
  28.9 6.0 %collective-permute-start.4 = (f32[2,1,256]{2,1,0:T(1,128)S(1)}, f32[2,1,256]{2,1,0:T(1,128)S(1)}, u32[]{:S(2)}, u32[]{:S(2)}) collective-permute-start(f32[2,1,256]{2,1,0:T(1,128)S(1)} %get-tuple-element.39), channel_id=1, source_target_pairs={{0,8},{8,16},{16,24},{24,32},{32,40},{40,48},{48,56},{56,64},{64,7... | collective-permute-start | bytes 6152 | tf_op jit(solution)/shard_map/ppermute | solution.py:27
  31.2 13.2 %copy-start.25 = (f32[256,2,128]{2,1,0:T(2,128)S(1)}, f32[256,2,128]{2,1,0:T(2,128)}, u32[]{:S(2)}) copy-start(f32[256,2,128]{2,1,0:T(2,128)} %copy-done.24) | copy-start | bytes 786436
  31.2 7.7 %collective-permute-start.5 = (f32[2,1,256]{2,1,0:T(1,128)S(1)}, f32[2,1,256]{2,1,0:T(1,128)S(1)}, u32[]{:S(2)}, u32[]{:S(2)}) collective-permute-start(f32[2,1,256]{2,1,0:T(1,128)S(1)} %get-tuple-element.40), channel_id=1, source_target_pairs={{8,0},{16,8},{24,16},{32,24},{40,32},{48,40},{56,48},{64,56},{72,6... | collective-permute-start | bytes 6152 | tf_op jit(solution)/shard_map/ppermute | solution.py:28
  39.1 9.2 %collective-permute-start.6 = (f32[2,258,1]{2,1,0:T(8,128)S(1)}, f32[2,258,1]{2,1,0:T(8,128)S(1)}, u32[]{:S(2)}, u32[]{:S(2)}) collective-permute-start(f32[2,258,1]{2,1,0:T(8,128)S(1)} %get-tuple-element.19), channel_id=1, source_target_pairs={{0,1},{1,2},{2,3},{3,4},{4,5},{5,6},{6,7},{7,128},{128,129},{129,1... | collective-permute-start | bytes 6200 | tf_op jit(solution)/shard_map/ppermute | solution.py:27
  42.9 10.1 %collective-permute-start.7 = (f32[2,258,1]{2,1,0:T(8,128)S(1)}, f32[2,258,1]{2,1,0:T(8,128)S(1)}, u32[]{:S(2)}, u32[]{:S(2)}) collective-permute-start(f32[2,258,1]{2,1,0:T(8,128)S(1)} %get-tuple-element.20), channel_id=1, source_target_pairs={{1,0},{2,1},{3,2},{4,3},{5,4},{6,5},{7,6},{128,7},{129,128},{130,1... | collective-permute-start | bytes 6200 | tf_op jit(solution)/shard_map/ppermute | solution.py:28
  44.4 44.4 %copy-start.3 = (f32[32,8,2,128]{3,1,2,0:T(8,128)}, f32[32,8,2,128]{3,1,2,0:T(8,128)S(1)}, u32[]{:S(2)}) copy-start(f32[32,8,2,128]{3,1,2,0:T(8,128)S(1)} %copy.140) | copy-start | bytes 786436
  53.9 0.7 copy-start.6
  54.4 1.1 copy-start.10
  61.1 1.0 copy-start.16
  65.0 5.9 %collective-permute-start.8 = (f32[2,1,256]{2,1,0:T(1,128)S(1)}, f32[2,1,256]{2,1,0:T(1,128)S(1)}, u32[]{:S(2)}, u32[]{:S(2)}) collective-permute-start(f32[2,1,256]{2,1,0:T(1,128)S(1)} %get-tuple-element.33), channel_id=1, source_target_pairs={{0,8},{8,16},{16,24},{24,32},{32,40},{40,48},{48,56},{56,64},{64,7... | collective-permute-start | bytes 6152 | tf_op jit(solution)/shard_map/ppermute | solution.py:27
  66.9 7.6 %collective-permute-start.9 = (f32[2,1,256]{2,1,0:T(1,128)S(1)}, f32[2,1,256]{2,1,0:T(1,128)S(1)}, u32[]{:S(2)}, u32[]{:S(2)}) collective-permute-start(f32[2,1,256]{2,1,0:T(1,128)S(1)} %get-tuple-element.34), channel_id=1, source_target_pairs={{8,0},{16,8},{24,16},{32,24},{40,32},{48,40},{56,48},{64,56},{72,6... | collective-permute-start | bytes 6152 | tf_op jit(solution)/shard_map/ppermute | solution.py:28
  74.7 8.2 %collective-permute-start.10 = (f32[2,258,1]{2,1,0:T(8,128)S(1)}, f32[2,258,1]{2,1,0:T(8,128)S(1)}, u32[]{:S(2)}, u32[]{:S(2)}) collective-permute-start(f32[2,258,1]{2,1,0:T(8,128)S(1)} %get-tuple-element.17), channel_id=1, source_target_pairs={{0,1},{1,2},{2,3},{3,4},{4,5},{5,6},{6,7},{7,128},{128,129},{129,1... | collective-permute-start | bytes 6200 | tf_op jit(solution)/shard_map/ppermute | solution.py:27
  77.9 9.4 %collective-permute-start.11 = (f32[2,258,1]{2,1,0:T(8,128)S(1)}, f32[2,258,1]{2,1,0:T(8,128)S(1)}, u32[]{:S(2)}, u32[]{:S(2)}) collective-permute-start(f32[2,258,1]{2,1,0:T(8,128)S(1)} %get-tuple-element.18), channel_id=1, source_target_pairs={{1,0},{2,1},{3,2},{4,3},{5,4},{6,5},{7,6},{128,7},{129,128},{130,1... | collective-permute-start | bytes 6200 | tf_op jit(solution)/shard_map/ppermute | solution.py:28
  88.3 0.7 copy-start.18
  88.4 1.4 copy-start.7
  88.4 1.4 copy-start.11
  89.1 0.7 copy-start.21
  96.3 1.0 copy-start.17
  100.2 6.1 %collective-permute-start.12 = (f32[2,1,256]{2,1,0:T(1,128)S(1)}, f32[2,1,256]{2,1,0:T(1,128)S(1)}, u32[]{:S(2)}, u32[]{:S(2)}) collective-permute-start(f32[2,1,256]{2,1,0:T(1,128)S(1)} %get-tuple-element.27), channel_id=1, source_target_pairs={{0,8},{8,16},{16,24},{24,32},{32,40},{40,48},{48,56},{56,64},{64,7... | collective-permute-start | bytes 6152 | tf_op jit(solution)/shard_map/ppermute | solution.py:27
  102.4 7.6 %collective-permute-start.13 = (f32[2,1,256]{2,1,0:T(1,128)S(1)}, f32[2,1,256]{2,1,0:T(1,128)S(1)}, u32[]{:S(2)}, u32[]{:S(2)}) collective-permute-start(f32[2,1,256]{2,1,0:T(1,128)S(1)} %get-tuple-element.28), channel_id=1, source_target_pairs={{8,0},{16,8},{24,16},{32,24},{40,32},{48,40},{56,48},{64,56},{72,6... | collective-permute-start | bytes 6152 | tf_op jit(solution)/shard_map/ppermute | solution.py:28
  110.1 9.1 %collective-permute-start.14 = (f32[2,258,1]{2,1,0:T(8,128)S(1)}, f32[2,258,1]{2,1,0:T(8,128)S(1)}, u32[]{:S(2)}, u32[]{:S(2)}) collective-permute-start(f32[2,258,1]{2,1,0:T(8,128)S(1)} %get-tuple-element.15), channel_id=1, source_target_pairs={{0,1},{1,2},{2,3},{3,4},{4,5},{5,6},{6,7},{7,128},{128,129},{129,1... | collective-permute-start | bytes 6200 | tf_op jit(solution)/shard_map/ppermute | solution.py:27
  115.3 8.4 %collective-permute-start.15 = (f32[2,258,1]{2,1,0:T(8,128)S(1)}, f32[2,258,1]{2,1,0:T(8,128)S(1)}, u32[]{:S(2)}, u32[]{:S(2)}) collective-permute-start(f32[2,258,1]{2,1,0:T(8,128)S(1)} %get-tuple-element.16), channel_id=1, source_target_pairs={{1,0},{2,1},{3,2},{4,3},{5,4},{6,5},{7,6},{128,7},{129,128},{130,1... | collective-permute-start | bytes 6200 | tf_op jit(solution)/shard_map/ppermute | solution.py:28
  124.6 0.7 copy-start.26
  124.6 1.4 copy-start.4
  124.6 1.4 copy-start.8
  124.6 1.4 copy-start.12
  124.6 1.4 copy-start.19
  124.7 1.4 copy-start.22
  125.3 0.7 copy-start.28
  132.6 1.0 copy-start.2
  132.6 1.1 copy-start.15
  136.5 5.9 %collective-permute-start.16 = (f32[2,1,256]{2,1,0:T(1,128)S(1)}, f32[2,1,256]{2,1,0:T(1,128)S(1)}, u32[]{:S(2)}, u32[]{:S(2)}) collective-permute-start(f32[2,1,256]{2,1,0:T(1,128)S(1)} %get-tuple-element.21), channel_id=1, source_target_pairs={{0,8},{8,16},{16,24},{24,32},{32,40},{40,48},{48,56},{56,64},{64,7... | collective-permute-start | bytes 6152 | tf_op jit(solution)/shard_map/ppermute | solution.py:27
  138.5 7.6 %collective-permute-start.17 = (f32[2,1,256]{2,1,0:T(1,128)S(1)}, f32[2,1,256]{2,1,0:T(1,128)S(1)}, u32[]{:S(2)}, u32[]{:S(2)}) collective-permute-start(f32[2,1,256]{2,1,0:T(1,128)S(1)} %get-tuple-element.22), channel_id=1, source_target_pairs={{8,0},{16,8},{24,16},{32,24},{40,32},{48,40},{56,48},{64,56},{72,6... | collective-permute-start | bytes 6152 | tf_op jit(solution)/shard_map/ppermute | solution.py:28
  146.2 7.9 %collective-permute-start.18 = (f32[2,258,1]{2,1,0:T(8,128)S(1)}, f32[2,258,1]{2,1,0:T(8,128)S(1)}, u32[]{:S(2)}, u32[]{:S(2)}) collective-permute-start(f32[2,258,1]{2,1,0:T(8,128)S(1)} %get-tuple-element.13), channel_id=1, source_target_pairs={{0,1},{1,2},{2,3},{3,4},{4,5},{5,6},{6,7},{7,128},{128,129},{129,1... | collective-permute-start | bytes 6200 | tf_op jit(solution)/shard_map/ppermute | solution.py:27
  150.2 8.4 %collective-permute-start.19 = (f32[2,258,1]{2,1,0:T(8,128)S(1)}, f32[2,258,1]{2,1,0:T(8,128)S(1)}, u32[]{:S(2)}, u32[]{:S(2)}) collective-permute-start(f32[2,258,1]{2,1,0:T(8,128)S(1)} %get-tuple-element.14), channel_id=1, source_target_pairs={{1,0},{2,1},{3,2},{4,3},{5,4},{6,5},{7,6},{128,7},{129,128},{130,1... | collective-permute-start | bytes 6200 | tf_op jit(solution)/shard_map/ppermute | solution.py:28
  159.5 1.0 copy-start.5
  159.5 1.0 copy-start.9
  159.5 1.1 copy-start.13
  159.5 1.2 copy-start.20
  159.5 1.2 copy-start.23
  159.5 1.3 copy-start.27
  159.5 1.4 copy-start.29
  164.8 1.4 collective-permute-start.20
  166.9 3.6 %collective-permute-start.21 = (f32[8,128]{1,0:T(8,128)S(1)}, f32[8,128]{1,0:T(8,128)S(1)}, u32[]{:S(2)}, u32[]{:S(2)}) collective-permute-start(f32[8,128]{1,0:T(8,128)S(1)} %add.457), channel_id=1, source_target_pairs={{0,8},{8,0},{16,24},{24,16},{32,40},{40,32},{48,56},{56,48},{64,72... | collective-permute-start | bytes 12296 | tf_op jit(solution)/shard_map/ppermute | solution.py:226
  170.5 5.1 %collective-permute-start.22 = (f32[8,128]{1,0:T(8,128)S(1)}, f32[8,128]{1,0:T(8,128)S(1)}, u32[]{:S(2)}, u32[]{:S(2)}) collective-permute-start(f32[8,128]{1,0:T(8,128)S(1)} %add.458), channel_id=1, source_target_pairs={{0,16},{8,24},{16,0},{24,8},{32,48},{40,56},{48,32},{56,40},{64,80... | collective-permute-start | bytes 12296 | tf_op jit(solution)/shard_map/ppermute | solution.py:226
  175.6 3.6 %collective-permute-start.23 = (f32[8,128]{1,0:T(8,128)S(1)}, f32[8,128]{1,0:T(8,128)S(1)}, u32[]{:S(2)}, u32[]{:S(2)}) collective-permute-start(f32[8,128]{1,0:T(8,128)S(1)} %add.459), channel_id=1, source_target_pairs={{0,32},{8,40},{16,48},{24,56},{32,0},{40,8},{48,16},{56,24},{64,96... | collective-permute-start | bytes 12296 | tf_op jit(solution)/shard_map/ppermute | solution.py:226
  179.2 5.1 %collective-permute-start.24 = (f32[8,128]{1,0:T(8,128)S(1)}, f32[8,128]{1,0:T(8,128)S(1)}, u32[]{:S(2)}, u32[]{:S(2)}) collective-permute-start(f32[8,128]{1,0:T(8,128)S(1)} %add.460), channel_id=1, source_target_pairs={{0,64},{8,72},{16,80},{24,88},{32,96},{40,104},{48,112},{56,120},{... | collective-permute-start | bytes 12296 | tf_op jit(solution)/shard_map/ppermute | solution.py:226
  184.4 3.6 %collective-permute-start.25 = (f32[8,128]{1,0:T(8,128)S(1)}, f32[8,128]{1,0:T(8,128)S(1)}, u32[]{:S(2)}, u32[]{:S(2)}) collective-permute-start(f32[8,128]{1,0:T(8,128)S(1)} %add.461), channel_id=1, source_target_pairs={{0,1},{1,0},{2,3},{3,2},{4,5},{5,4},{6,7},{7,6},{8,9},{9,8},{10,11... | collective-permute-start | bytes 12296 | tf_op jit(solution)/shard_map/ppermute | solution.py:226
  188.0 4.5 %collective-permute-start.26 = (f32[8,128]{1,0:T(8,128)S(1)}, f32[8,128]{1,0:T(8,128)S(1)}, u32[]{:S(2)}, u32[]{:S(2)}) collective-permute-start(f32[8,128]{1,0:T(8,128)S(1)} %add.462), channel_id=1, source_target_pairs={{0,2},{1,3},{2,0},{3,1},{4,6},{5,7},{6,4},{7,5},{8,10},{9,11},{10,... | collective-permute-start | bytes 12296 | tf_op jit(solution)/shard_map/ppermute | solution.py:226
  192.5 7.5 %collective-permute-start.27 = (f32[8,128]{1,0:T(8,128)S(1)}, f32[8,128]{1,0:T(8,128)S(1)}, u32[]{:S(2)}, u32[]{:S(2)}) collective-permute-start(f32[8,128]{1,0:T(8,128)S(1)} %add.463), channel_id=1, source_target_pairs={{0,4},{1,5},{2,6},{3,7},{4,0},{5,1},{6,2},{7,3},{8,12},{9,13},{10,... | collective-permute-start | bytes 12296 | tf_op jit(solution)/shard_map/ppermute | solution.py:226
where the time goes:
time: 209 us; the launch traced here: 207 us
  waiting for transfers between devices  71.7 us (34%)
  starting transfers between devices  68.9 us (33%)
  local copies, waits for them, and re-layouts  34.2 us (16%)
  other arithmetic  26.7 us (13%)
  Pallas kernels  4.71 us (2%)
    ppermute x10, starting transfers between devices, edges(): before = lax.ppermute(last, axis, up)  34.9 us
    ppermute x10, waiting for transfers between devices, edges(): after = lax.ppermute(initial, axis, down)  33.5 us
    ppermute x8, waiting for transfers between devices, butterfly(): lax.ppermute(values, axis, [(i, i ^ stride) for i in range(size)])  25.3 us
    ppermute x10, starting transfers between devices, edges(): after = lax.ppermute(initial, axis, down)  24.9 us
    ppermute x10, waiting for transfers between devices, edges(): before = lax.ppermute(last, axis, up)  12.8 us
    ppermute x8, starting transfers between devices, butterfly(): lax.ppermute(values, axis, [(i, i ^ stride) for i in range(size)])  9.11 us
    reshape x4, local copies, waits for them, and re-layouts, grid_to_blocks(): tile_grid.reshape(channels, tile_rows // BS, BS, tile_cols // BS, BS)  6.57 us
    unnamed x69, local copies, waits for them, and re-layouts  5.31 us
  transfers between devices with their start and end apart: 28, of which 21 were waited for; matrix products, arithmetic and copies ran while one was open for 3% of the time, Pallas kernels for 0%

commit v1 on v0

--- a/solution.py
+++ b/solution.py
@@ -64,29 +64,57 @@
     return jnp.stack([along_u, along_v], axis=-3)
 
 
-def grid_to_blocks(tile_grid):
-    channels, tile_rows, tile_cols = tile_grid.shape
-    shaped = tile_grid.reshape(channels, tile_rows // BS, BS, tile_cols // BS, BS).transpose(
-        1, 3, 0, 2, 4
-    )
-    return shaped.reshape(tile_rows // BS * (tile_cols // BS), channels, BS, BS)
-
-
-def blocks_to_grid(blocks, tile_rows, tile_cols):
-    channels = blocks.shape[1]
-    shaped = blocks.reshape(tile_rows // BS, tile_cols // BS, channels, BS, BS).transpose(
-        2, 0, 3, 1, 4
-    )
-    return shaped.reshape(channels, tile_rows, tile_cols)
-
-
-def precondition(vector, zeta_blocks, diag_blocks):
-    diagonal_total = (diag_blocks + 3.0 * zeta_blocks)[:, None]
+def block_stencil(field, zeta_field, diag_field):
+    rows = lax.broadcasted_iota(jnp.int32, field.shape[-2:], 0) % BS
+    cols = lax.broadcasted_iota(jnp.int32, field.shape[-2:], 1) % BS
+    padded = jnp.pad(field, ((0, 0), (1, 1), (1, 1)))
+    height, width = field.shape[-2:]
+
+    def neighbour(di, dj):
+        inside = jnp.ones(field.shape[-2:], jnp.bool_)
+        if di:
+            inside = inside & (rows != (BS - 1 if di > 0 else 0))
+        if dj:
+            inside = inside & (cols != (BS - 1 if dj > 0 else 0))
+        window = padded[:, 1 + di : 1 + di + height, 1 + dj : 1 + dj + width]
+        return jnp.where(inside, window, 0.0)
+
+    def pieces(channel):
+        center = field[channel]
+        second_x = neighbour(1, 0)[channel] + neighbour(-1, 0)[channel] - 2.0 * center
+        second_y = neighbour(0, 1)[channel] + neighbour(0, -1)[channel] - 2.0 * center
+        mixed = 0.25 * (
+            neighbour(1, 1)[channel]
+            - neighbour(1, -1)[channel]
+            - neighbour(-1, 1)[channel]
+            + neighbour(-1, -1)[channel]
+        )
+        return (center, second_x, second_y, mixed)
+
+    part_u = pieces(0)
+    part_v = pieces(1)
+    along_u = (
+        diag_field * part_u[0]
+        - 1.25 * zeta_field * part_u[1]
+        - 0.25 * zeta_field * part_u[2]
+        - zeta_field * part_v[3]
+    )
+    along_v = (
+        diag_field * part_v[0]
+        - 0.25 * zeta_field * part_v[1]
+        - 1.25 * zeta_field * part_v[2]
+        - zeta_field * part_u[3]
+    )
+    return jnp.stack([along_u, along_v], axis=0)
+
+
+def precondition(vector, zeta_field, diag_field):
+    diagonal_total = diag_field + 3.0 * zeta_field
     iterate = vector / diagonal_total
     for relaxation in range(SWEEPS):
-        padded = jnp.pad(iterate, ((0, 0), (0, 0), (1, 1), (1, 1)))
         iterate = (
-            iterate + RELAX * (vector - stencil(padded, zeta_blocks, diag_blocks)) / diagonal_total
+            iterate
+            + RELAX * (vector - block_stencil(iterate, zeta_field, diag_field)) / diagonal_total
         )
     return iterate
 
@@ -269,16 +297,12 @@
     )
     rhs = live * is_ocean * (surface_stress + mass_term * old_velocity)
 
-    zeta_blocks = grid_to_blocks(zeta_tile[None])[:, 0]
-    diag_blocks = grid_to_blocks(diag_tile[None])[:, 0]
 
     def apply_system(vector):
         return live * stencil(extended(vector), zeta_tile, diag_tile)
 
     def apply_precond(vector):
-        return blocks_to_grid(
-            precondition(grid_to_blocks(vector), zeta_blocks, diag_blocks), tile_rows, tile_cols
-        )
+        return precondition(vector, zeta_tile, diag_tile)
 
     krylov = [rhs]
     directions = []

time: 209 us -> 188 us (0.90)
  local copies, waits for them, and re-layouts: 34.2 us -> 10.4 us
    reshape x12 -> x0, local copies, waits for them, and re-layouts: 14.6 us -> none  [the longest x4 6.57 us: grid_to_blocks(): tile_grid.reshape(channels, tile_rows // BS, BS, tile_cols // BS, BS)]
    sub x16 -> x0, other arithmetic: 7.8 us -> none  [the longest x8 3.9 us: stencil(): diag_field * part_v[0] - 0.25 * zeta_field * part_v[1]]
    select_n x0 -> x8, other arithmetic: none -> 7.73 us  [neighbour(): return jnp.where(inside, window, 0.0)]
    transpose x6 -> x0, local copies, waits for them, and re-layouts: 4.07 us -> none  [the longest x4 4.03 us: blocks_to_grid(): blocks.reshape(tile_rows // BS, tile_cols // BS, channels, BS, BS)]
    another operation x0 -> x16, other arithmetic: none -> 3.11 us  [block_stencil(): return jnp.stack([along_u, along_v], axis=0)]
    sub x4 -> x1, other arithmetic: 3.75 us -> 0.88 us  [shards(): krylov.append(apply_system(directions[-1]) - SHIFT * krylov[-1])]
    squeeze x12 -> x4, local copies, waits for them, and re-layouts: 3.04 us -> 0.22 us  [stencil(): part_v = pieces(padded[..., 1, :, :])]
    add x1, other arithmetic: 3.41 us -> 5.87 us  [shards(): solution = solution + update[i] * directions[i]]
  transfers between devices with their start and end apart: 28 -> 28, of which waited for: 21 -> 22; matrix products, arithmetic and copies ran while one was open for 3% -> 1% of each run, Pallas kernels for 0% -> 0%
where the time goes in v1:
time: 188 us; the launch traced here: 187 us
  waiting for transfers between devices  73.6 us (39%)
  starting transfers between devices  69.3 us (37%)
  other arithmetic  28.4 us (15%)
  local copies, waits for them, and re-layouts  10.4 us (6%)
  Pallas kernels  4.86 us (3%)
    ppermute x10, waiting for transfers between devices, edges(): after = lax.ppermute(initial, axis, down)  35.7 us
    ppermute x10, starting transfers between devices, edges(): before = lax.ppermute(last, axis, up)  35.3 us
    ppermute x8, waiting for transfers between devices, butterfly(): lax.ppermute(values, axis, [(i, i ^ stride) for i in range(size)])  25.3 us
    ppermute x10, starting transfers between devices, edges(): after = lax.ppermute(initial, axis, down)  24.9 us
    ppermute x10, waiting for transfers between devices, edges(): before = lax.ppermute(last, axis, up)  12.5 us
    ppermute x8, starting transfers between devices, butterfly(): lax.ppermute(values, axis, [(i, i ^ stride) for i in range(size)])  9.11 us
    select_n x8, other arithmetic, neighbour(): return jnp.where(inside, window, 0.0)  7.73 us
    add x1, other arithmetic, shards(): solution = solution + update[i] * directions[i]  5.87 us
  transfers between devices with their start and end apart: 28, of which 22 were waited for; matrix products, arithmetic and copies ran while one was open for 1% of the time, Pallas kernels for 0%

profile of v1, /device:TPU:24, one launch (start us, length us, event | category | flops | bytes accessed | tf_op | source)
XLA Modules:
  0.0 187.4 jit_solution(10338210187810012509)
XLA Ops:
  0.0 0.7 fusion.410
  0.7 2.6 %collective-permute-start = (f32[2,1,256]{2,1,0:T(1,128)S(1)}, f32[2,1,256]{2,1,0:T(1,128)S(1)}, u32[]{:S(2)}, u32[]{:S(2)}) collective-permute-start(f32[2,1,256]{2,1,0:T(1,128)S(1)} %get-tuple-element.108), channel_id=1, source_target_pairs={{8,0},{16,8},{24,16},{32,24},{40,32},{48,40},{56,48},{64,56},{72,6... | collective-permute-start | bytes 6152 | tf_op jit(solution)/shard_map/ppermute | solution.py:28
  3.4 5.4 %collective-permute-start.1 = (f32[2,1,256]{2,1,0:T(1,128)S(1)}, f32[2,1,256]{2,1,0:T(1,128)S(1)}, u32[]{:S(2)}, u32[]{:S(2)}) collective-permute-start(f32[2,1,256]{2,1,0:T(1,128)S(1)} %get-tuple-element.109), channel_id=1, source_target_pairs={{0,8},{8,16},{16,24},{24,32},{32,40},{40,48},{48,56},{56,64},{64,7... | collective-permute-start | bytes 6152 | tf_op jit(solution)/shard_map/ppermute | solution.py:27
  8.8 1.9 fusion.409
  10.7 1.3 collective-permute-start.2
  12.0 5.3 %collective-permute-start.3 = (f32[2,256,1]{2,1,0:T(8,128)}, f32[2,256,1]{2,1,0:T(8,128)}, u32[]{:S(2)}, u32[]{:S(2)}) collective-permute-start(f32[2,256,1]{2,1,0:T(8,128)} %get-tuple-element.105), channel_id=1, source_target_pairs={{0,1},{1,2},{2,3},{3,4},{4,5},{5,6},{6,7},{7,128},{128,129},{129,1... | collective-permute-start | bytes 6152 | tf_op jit(solution)/shard_map/ppermute | solution.py:27
  17.6 0.6 copy-done.31
  18.6 1.7 collective-permute-done.2
  21.5 1.6 multiply_add_fusion.1
  23.2 1.0 fusion
  24.7 1.0 fusion.8
  27.3 2.2 %collective-permute-start.4 = (f32[2,1,256]{2,1,0:T(1,128)S(1)}, f32[2,1,256]{2,1,0:T(1,128)S(1)}, u32[]{:S(2)}, u32[]{:S(2)}) collective-permute-start(f32[2,1,256]{2,1,0:T(1,128)S(1)} %get-tuple-element.86), channel_id=1, source_target_pairs={{0,8},{8,16},{16,24},{24,32},{32,40},{40,48},{48,56},{56,64},{64,7... | collective-permute-start | bytes 6152 | tf_op jit(solution)/shard_map/ppermute | solution.py:27
  29.5 3.6 %collective-permute-start.5 = (f32[2,1,256]{2,1,0:T(1,128)S(1)}, f32[2,1,256]{2,1,0:T(1,128)S(1)}, u32[]{:S(2)}, u32[]{:S(2)}) collective-permute-start(f32[2,1,256]{2,1,0:T(1,128)S(1)} %get-tuple-element.87), channel_id=1, source_target_pairs={{8,0},{16,8},{24,16},{32,24},{40,32},{48,40},{56,48},{64,56},{72,6... | collective-permute-start | bytes 6152 | tf_op jit(solution)/shard_map/ppermute | solution.py:28
  33.2 3.9 %collective-permute-done.5 = f32[2,1,256]{2,1,0:T(1,128)S(1)} collective-permute-done((f32[2,1,256]{2,1,0:T(1,128)S(1)}, f32[2,1,256]{2,1,0:T(1,128)S(1)}, u32[]{:S(2)}, u32[]{:S(2)}) %collective-permute-start.5) | collective-permute-done | bytes 2080 | tf_op jit(solution)/shard_map/ppermute | solution.py:28
  37.3 4.5 %collective-permute-start.6 = (f32[2,258,1]{2,1,0:T(8,128)S(1)}, f32[2,258,1]{2,1,0:T(8,128)S(1)}, u32[]{:S(2)}, u32[]{:S(2)}) collective-permute-start(f32[2,258,1]{2,1,0:T(8,128)S(1)} %get-tuple-element.30), channel_id=1, source_target_pairs={{0,1},{1,2},{2,3},{3,4},{4,5},{5,6},{6,7},{7,128},{128,129},{129,1... | collective-permute-start | bytes 6200 | tf_op jit(solution)/shard_map/ppermute | solution.py:27
  41.8 1.3 collective-permute-start.7
  43.2 3.4 %collective-permute-done.6 = f32[2,258,1]{2,1,0:T(8,128)S(1)} collective-permute-done((f32[2,258,1]{2,1,0:T(8,128)S(1)}, f32[2,258,1]{2,1,0:T(8,128)S(1)}, u32[]{:S(2)}, u32[]{:S(2)}) %collective-permute-start.6) | collective-permute-done | bytes 2096 | tf_op jit(solution)/shard_map/ppermute | solution.py:27
  46.6 5.6 %collective-permute-done.7 = f32[2,258,1]{2,1,0:T(8,128)S(1)} collective-permute-done((f32[2,258,1]{2,1,0:T(8,128)S(1)}, f32[2,258,1]{2,1,0:T(8,128)S(1)}, u32[]{:S(2)}, u32[]{:S(2)}) %collective-permute-start.7) | collective-permute-done | bytes 2096 | tf_op jit(solution)/shard_map/ppermute | solution.py:28
  53.8 1.0 fusion.16
  55.3 1.0 fusion.24
  57.9 1.9 %collective-permute-start.8 = (f32[2,1,256]{2,1,0:T(1,128)S(1)}, f32[2,1,256]{2,1,0:T(1,128)S(1)}, u32[]{:S(2)}, u32[]{:S(2)}) collective-permute-start(f32[2,1,256]{2,1,0:T(1,128)S(1)} %get-tuple-element.68), channel_id=1, source_target_pairs={{0,8},{8,16},{16,24},{24,32},{32,40},{40,48},{48,56},{56,64},{64,7... | collective-permute-start | bytes 6152 | tf_op jit(solution)/shard_map/ppermute | solution.py:27
  59.8 3.9 %collective-permute-start.9 = (f32[2,1,256]{2,1,0:T(1,128)S(1)}, f32[2,1,256]{2,1,0:T(1,128)S(1)}, u32[]{:S(2)}, u32[]{:S(2)}) collective-permute-start(f32[2,1,256]{2,1,0:T(1,128)S(1)} %get-tuple-element.69), channel_id=1, source_target_pairs={{8,0},{16,8},{24,16},{32,24},{40,32},{48,40},{56,48},{64,56},{72,6... | collective-permute-start | bytes 6152 | tf_op jit(solution)/shard_map/ppermute | solution.py:28
  63.8 3.6 %collective-permute-done.9 = f32[2,1,256]{2,1,0:T(1,128)S(1)} collective-permute-done((f32[2,1,256]{2,1,0:T(1,128)S(1)}, f32[2,1,256]{2,1,0:T(1,128)S(1)}, u32[]{:S(2)}, u32[]{:S(2)}) %collective-permute-start.9) | collective-permute-done | bytes 2080 | tf_op jit(solution)/shard_map/ppermute | solution.py:28
  67.6 3.1 %collective-permute-start.10 = (f32[2,258,1]{2,1,0:T(8,128)S(1)}, f32[2,258,1]{2,1,0:T(8,128)S(1)}, u32[]{:S(2)}, u32[]{:S(2)}) collective-permute-start(f32[2,258,1]{2,1,0:T(8,128)S(1)} %get-tuple-element.28), channel_id=1, source_target_pairs={{0,1},{1,2},{2,3},{3,4},{4,5},{5,6},{6,7},{7,128},{128,129},{129,1... | collective-permute-start | bytes 6200 | tf_op jit(solution)/shard_map/ppermute | solution.py:27
  70.7 1.5 collective-permute-start.11
  72.1 3.7 %collective-permute-done.10 = f32[2,258,1]{2,1,0:T(8,128)S(1)} collective-permute-done((f32[2,258,1]{2,1,0:T(8,128)S(1)}, f32[2,258,1]{2,1,0:T(8,128)S(1)}, u32[]{:S(2)}, u32[]{:S(2)}) %collective-permute-start.10) | collective-permute-done | bytes 2096 | tf_op jit(solution)/shard_map/ppermute | solution.py:27
  75.8 4.7 %collective-permute-done.11 = f32[2,258,1]{2,1,0:T(8,128)S(1)} collective-permute-done((f32[2,258,1]{2,1,0:T(8,128)S(1)}, f32[2,258,1]{2,1,0:T(8,128)S(1)}, u32[]{:S(2)}, u32[]{:S(2)}) %collective-permute-start.11) | collective-permute-done | bytes 2096 | tf_op jit(solution)/shard_map/ppermute | solution.py:28
  82.1 1.0 fusion.32
  83.6 1.0 fusion.40
  86.3 1.9 %collective-permute-start.12 = (f32[2,1,256]{2,1,0:T(1,128)S(1)}, f32[2,1,256]{2,1,0:T(1,128)S(1)}, u32[]{:S(2)}, u32[]{:S(2)}) collective-permute-start(f32[2,1,256]{2,1,0:T(1,128)S(1)} %get-tuple-element.50), channel_id=1, source_target_pairs={{0,8},{8,16},{16,24},{24,32},{32,40},{40,48},{48,56},{56,64},{64,7... | collective-permute-start | bytes 6152 | tf_op jit(solution)/shard_map/ppermute | solution.py:27
  88.2 3.9 %collective-permute-start.13 = (f32[2,1,256]{2,1,0:T(1,128)S(1)}, f32[2,1,256]{2,1,0:T(1,128)S(1)}, u32[]{:S(2)}, u32[]{:S(2)}) collective-permute-start(f32[2,1,256]{2,1,0:T(1,128)S(1)} %get-tuple-element.51), channel_id=1, source_target_pairs={{8,0},{16,8},{24,16},{32,24},{40,32},{48,40},{56,48},{64,56},{72,6... | collective-permute-start | bytes 6152 | tf_op jit(solution)/shard_map/ppermute | solution.py:28
  92.1 3.6 %collective-permute-done.13 = f32[2,1,256]{2,1,0:T(1,128)S(1)} collective-permute-done((f32[2,1,256]{2,1,0:T(1,128)S(1)}, f32[2,1,256]{2,1,0:T(1,128)S(1)}, u32[]{:S(2)}, u32[]{:S(2)}) %collective-permute-start.13) | collective-permute-done | bytes 2080 | tf_op jit(solution)/shard_map/ppermute | solution.py:28
  95.9 5.1 %collective-permute-start.14 = (f32[2,258,1]{2,1,0:T(8,128)S(1)}, f32[2,258,1]{2,1,0:T(8,128)S(1)}, u32[]{:S(2)}, u32[]{:S(2)}) collective-permute-start(f32[2,258,1]{2,1,0:T(8,128)S(1)} %get-tuple-element.26), channel_id=1, source_target_pairs={{0,1},{1,2},{2,3},{3,4},{4,5},{5,6},{6,7},{7,128},{128,129},{129,1... | collective-permute-start | bytes 6200 | tf_op jit(solution)/shard_map/ppermute | solution.py:27
  101.1 1.3 collective-permute-start.15
  102.4 2.6 %collective-permute-done.14 = f32[2,258,1]{2,1,0:T(8,128)S(1)} collective-permute-done((f32[2,258,1]{2,1,0:T(8,128)S(1)}, f32[2,258,1]{2,1,0:T(8,128)S(1)}, u32[]{:S(2)}, u32[]{:S(2)}) %collective-permute-start.14) | collective-permute-done | bytes 2096 | tf_op jit(solution)/shard_map/ppermute | solution.py:27
  105.0 4.4 %collective-permute-done.15 = f32[2,258,1]{2,1,0:T(8,128)S(1)} collective-permute-done((f32[2,258,1]{2,1,0:T(8,128)S(1)}, f32[2,258,1]{2,1,0:T(8,128)S(1)}, u32[]{:S(2)}, u32[]{:S(2)}) %collective-permute-start.15) | collective-permute-done | bytes 2096 | tf_op jit(solution)/shard_map/ppermute | solution.py:28
  111.0 1.0 fusion.48
  112.6 1.0 fusion.56
  115.1 1.9 %collective-permute-start.16 = (f32[2,1,256]{2,1,0:T(1,128)S(1)}, f32[2,1,256]{2,1,0:T(1,128)S(1)}, u32[]{:S(2)}, u32[]{:S(2)}) collective-permute-start(f32[2,1,256]{2,1,0:T(1,128)S(1)} %get-tuple-element.32), channel_id=1, source_target_pairs={{0,8},{8,16},{16,24},{24,32},{32,40},{40,48},{48,56},{56,64},{64,7... | collective-permute-start | bytes 6152 | tf_op jit(solution)/shard_map/ppermute | solution.py:27
  117.1 3.9 %collective-permute-start.17 = (f32[2,1,256]{2,1,0:T(1,128)S(1)}, f32[2,1,256]{2,1,0:T(1,128)S(1)}, u32[]{:S(2)}, u32[]{:S(2)}) collective-permute-start(f32[2,1,256]{2,1,0:T(1,128)S(1)} %get-tuple-element.33), channel_id=1, source_target_pairs={{8,0},{16,8},{24,16},{32,24},{40,32},{48,40},{56,48},{64,56},{72,6... | collective-permute-start | bytes 6152 | tf_op jit(solution)/shard_map/ppermute | solution.py:28
  121.0 3.6 %collective-permute-done.17 = f32[2,1,256]{2,1,0:T(1,128)S(1)} collective-permute-done((f32[2,1,256]{2,1,0:T(1,128)S(1)}, f32[2,1,256]{2,1,0:T(1,128)S(1)}, u32[]{:S(2)}, u32[]{:S(2)}) %collective-permute-start.17) | collective-permute-done | bytes 2080 | tf_op jit(solution)/shard_map/ppermute | solution.py:28
  124.8 3.9 %collective-permute-start.18 = (f32[2,258,1]{2,1,0:T(8,128)S(1)}, f32[2,258,1]{2,1,0:T(8,128)S(1)}, u32[]{:S(2)}, u32[]{:S(2)}) collective-permute-start(f32[2,258,1]{2,1,0:T(8,128)S(1)} %get-tuple-element.24), channel_id=1, source_target_pairs={{0,1},{1,2},{2,3},{3,4},{4,5},{5,6},{6,7},{7,128},{128,129},{129,1... | collective-permute-start | bytes 6200 | tf_op jit(solution)/shard_map/ppermute | solution.py:27
  128.8 1.5 collective-permute-start.19
  130.3 2.4 %collective-permute-done.18 = f32[2,258,1]{2,1,0:T(8,128)S(1)} collective-permute-done((f32[2,258,1]{2,1,0:T(8,128)S(1)}, f32[2,258,1]{2,1,0:T(8,128)S(1)}, u32[]{:S(2)}, u32[]{:S(2)}) %collective-permute-start.18) | collective-permute-done | bytes 2096 | tf_op jit(solution)/shard_map/ppermute | solution.py:27
  132.7 4.4 %collective-permute-done.19 = f32[2,258,1]{2,1,0:T(8,128)S(1)} collective-permute-done((f32[2,258,1]{2,1,0:T(8,128)S(1)}, f32[2,258,1]{2,1,0:T(8,128)S(1)}, u32[]{:S(2)}, u32[]{:S(2)}) %collective-permute-start.19) | collective-permute-done | bytes 2096 | tf_op jit(solution)/shard_map/ppermute | solution.py:28
  138.6 0.9 fusion.91
  139.5 3.1 %shard_map.82 = f32[8,128]{1,0:T(8,128)} custom-call(f32[512,256]{1,0:T(8,128)} %bitcast.601, f32[512,256]{1,0:T(8,128)} %bitcast.598, f32[512,256]{1,0:T(8,128)} %bitcast.599, f32[512,256]{1,0:T(8,128)} %bitcast.600, f32[512,256]{1,0:T(8,128)} %bitcast.608), custom_call_target="tpu_custom_call" | custom-call | tf_op jit(solution)/shard_map/pallas_call | solution.py:215
  142.6 1.4 collective-permute-done.20
  144.0 0.7 add.734
  144.7 3.6 %collective-permute-done.21 = f32[8,128]{1,0:T(8,128)S(1)} collective-permute-done((f32[8,128]{1,0:T(8,128)S(1)}, f32[8,128]{1,0:T(8,128)S(1)}, u32[]{:S(2)}, u32[]{:S(2)}) %collective-permute-start.21) | collective-permute-done | bytes 4128 | tf_op jit(solution)/shard_map/ppermute | solution.py:254
  148.3 5.1 %collective-permute-done.22 = f32[8,128]{1,0:T(8,128)S(1)} collective-permute-done((f32[8,128]{1,0:T(8,128)S(1)}, f32[8,128]{1,0:T(8,128)S(1)}, u32[]{:S(2)}, u32[]{:S(2)}) %collective-permute-start.22) | collective-permute-done | bytes 4128 | tf_op jit(solution)/shard_map/ppermute | solution.py:254
  153.4 1.5 collective-permute-start.23
  154.9 2.1 %collective-permute-done.23 = f32[8,128]{1,0:T(8,128)S(1)} collective-permute-done((f32[8,128]{1,0:T(8,128)S(1)}, f32[8,128]{1,0:T(8,128)S(1)}, u32[]{:S(2)}, u32[]{:S(2)}) %collective-permute-start.23) | collective-permute-done | bytes 4128 | tf_op jit(solution)/shard_map/ppermute | solution.py:254
  157.0 3.0 %collective-permute-start.24 = (f32[8,128]{1,0:T(8,128)S(1)}, f32[8,128]{1,0:T(8,128)S(1)}, u32[]{:S(2)}, u32[]{:S(2)}) collective-permute-start(f32[8,128]{1,0:T(8,128)S(1)} %add.737), channel_id=1, source_target_pairs={{0,64},{8,72},{16,80},{24,88},{32,96},{40,104},{48,112},{56,120},{... | collective-permute-start | bytes 12296 | tf_op jit(solution)/shard_map/ppermute | solution.py:254
  160.0 2.1 %collective-permute-done.24 = f32[8,128]{1,0:T(8,128)S(1)} collective-permute-done((f32[8,128]{1,0:T(8,128)S(1)}, f32[8,128]{1,0:T(8,128)S(1)}, u32[]{:S(2)}, u32[]{:S(2)}) %collective-permute-start.24) | collective-permute-done | bytes 4128 | tf_op jit(solution)/shard_map/ppermute | solution.py:254
  162.1 1.2 collective-permute-start.25
  163.3 2.4 %collective-permute-done.25 = f32[8,128]{1,0:T(8,128)S(1)} collective-permute-done((f32[8,128]{1,0:T(8,128)S(1)}, f32[8,128]{1,0:T(8,128)S(1)}, u32[]{:S(2)}, u32[]{:S(2)}) %collective-permute-start.25) | collective-permute-done | bytes 4128 | tf_op jit(solution)/shard_map/ppermute | solution.py:254
  165.7 1.9 collective-permute-start.26
  167.6 2.6 %collective-permute-done.26 = f32[8,128]{1,0:T(8,128)S(1)} collective-permute-done((f32[8,128]{1,0:T(8,128)S(1)}, f32[8,128]{1,0:T(8,128)S(1)}, u32[]{:S(2)}, u32[]{:S(2)}) %collective-permute-start.26) | collective-permute-done | bytes 4128 | tf_op jit(solution)/shard_map/ppermute | solution.py:254
  170.2 1.5 collective-permute-start.27
  171.7 6.0 %collective-permute-done.27 = f32[8,128]{1,0:T(8,128)S(1)} collective-permute-done((f32[8,128]{1,0:T(8,128)S(1)}, f32[8,128]{1,0:T(8,128)S(1)}, u32[]{:S(2)}, u32[]{:S(2)}) %collective-permute-start.27) | collective-permute-done | bytes 4128 | tf_op jit(solution)/shard_map/ppermute | solution.py:254
  178.3 1.7 shard_map.83
  180.1 1.4 fusion.411
  181.6 5.9 %multiply_add_fusion = f32[2,256,256]{2,1,0:T(8,128)} fusion(f32[]{:T(128)} %bitcast.107, f32[]{:T(128)} %bitcast.106, f32[]{:T(128)} %bitcast.105, f32[]{:T(128)} %bitcast.104, f32[2,256,256]{2,1,0:T(8,128)S(1)} %copy-done.5, f32[1,256,256]{2,1,0:T(8,128)} %copy-done.23, f32[1,256,256]{2,1,0:T(8,128)} %copy-done.24, f32[1,256,256]{2,1,0:T(8,128)} %copy-done.15, ...), kind=kLoop, calls=%fused_computation.176 | loop fusion | flops 6684672 | bytes 7077904 | tf_op jit(solution)/shard_map/add | solution.py:316
  (149 shorter events, 17.7 us)
Async XLA Ops:
  0.7 19.6 %collective-permute-start = (f32[2,1,256]{2,1,0:T(1,128)S(1)}, f32[2,1,256]{2,1,0:T(1,128)S(1)}, u32[]{:S(2)}, u32[]{:S(2)}) collective-permute-start(f32[2,1,256]{2,1,0:T(1,128)S(1)} %get-tuple-element.108), channel_id=1, source_target_pairs={{8,0},{16,8},{24,16},{32,24},{40,32},{48,40},{56,48},{64,56},{72,6... | collective-permute-start | bytes 6152 | tf_op jit(solution)/shard_map/ppermute | solution.py:28
  3.4 13.9 %copy-start.8 = (f32[2,256,256]{2,1,0:T(8,128)S(1)}, f32[2,256,256]{2,1,0:T(8,128)}, u32[]{:S(2)}) copy-start(f32[2,256,256]{2,1,0:T(8,128)} %param.8) | copy-start | bytes 1572868
  3.4 17.0 %collective-permute-start.1 = (f32[2,1,256]{2,1,0:T(1,128)S(1)}, f32[2,1,256]{2,1,0:T(1,128)S(1)}, u32[]{:S(2)}, u32[]{:S(2)}) collective-permute-start(f32[2,1,256]{2,1,0:T(1,128)S(1)} %get-tuple-element.109), channel_id=1, source_target_pairs={{0,8},{8,16},{16,24},{24,32},{32,40},{40,48},{48,56},{56,64},{64,7... | collective-permute-start | bytes 6152 | tf_op jit(solution)/shard_map/ppermute | solution.py:27
  10.7 9.6 %collective-permute-start.2 = (f32[2,256,1]{2,1,0:T(8,128)S(1)}, f32[2,256,1]{2,1,0:T(8,128)S(1)}, u32[]{:S(2)}, u32[]{:S(2)}) collective-permute-start(f32[2,256,1]{2,1,0:T(8,128)S(1)} %get-tuple-element.104), channel_id=1, source_target_pairs={{1,0},{2,1},{3,2},{4,3},{5,4},{6,5},{7,6},{128,7},{129,128},{130,1... | collective-permute-start | bytes 6152 | tf_op jit(solution)/shard_map/ppermute | solution.py:28
  12.0 8.7 %collective-permute-start.3 = (f32[2,256,1]{2,1,0:T(8,128)}, f32[2,256,1]{2,1,0:T(8,128)}, u32[]{:S(2)}, u32[]{:S(2)}) collective-permute-start(f32[2,256,1]{2,1,0:T(8,128)} %get-tuple-element.105), channel_id=1, source_target_pairs={{0,1},{1,2},{2,3},{3,4},{4,5},{5,6},{6,7},{7,128},{128,129},{129,1... | collective-permute-start | bytes 6152 | tf_op jit(solution)/shard_map/ppermute | solution.py:27
  17.4 3.7 %copy-start.30 = (s32[256,256]{1,0:T(8,128)S(1)}, s32[256,256]{1,0:T(8,128)}, u32[]{:S(2)}) copy-start(s32[256,256]{1,0:T(8,128)} %param.13) | copy-start | bytes 786436
  17.6 0.7 copy-start.31
  20.3 1.0 copy-start.28
  20.3 1.0 copy-start.29
  20.3 1.0 copy-start.25
  20.4 1.1 copy-start.27
  21.5 1.6 copy-start.26
  23.2 30.4 %copy-start.6 = (f32[2,256,256]{2,1,0:T(8,128)}, f32[2,256,256]{2,1,0:T(8,128)S(1)}, u32[]{:S(2)}) copy-start(f32[2,256,256]{2,1,0:T(8,128)S(1)} %get-tuple-element.12) | copy-start | bytes 1572868
  25.9 0.7 copy-start.17
  26.6 0.7 copy-start.18
  27.3 5.8 %collective-permute-start.4 = (f32[2,1,256]{2,1,0:T(1,128)S(1)}, f32[2,1,256]{2,1,0:T(1,128)S(1)}, u32[]{:S(2)}, u32[]{:S(2)}) collective-permute-start(f32[2,1,256]{2,1,0:T(1,128)S(1)} %get-tuple-element.86), channel_id=1, source_target_pairs={{0,8},{8,16},{16,24},{24,32},{32,40},{40,48},{48,56},{56,64},{64,7... | collective-permute-start | bytes 6152 | tf_op jit(solution)/shard_map/ppermute | solution.py:27
  29.5 7.6 %collective-permute-start.5 = (f32[2,1,256]{2,1,0:T(1,128)S(1)}, f32[2,1,256]{2,1,0:T(1,128)S(1)}, u32[]{:S(2)}, u32[]{:S(2)}) collective-permute-start(f32[2,1,256]{2,1,0:T(1,128)S(1)} %get-tuple-element.87), channel_id=1, source_target_pairs={{8,0},{16,8},{24,16},{32,24},{40,32},{48,40},{56,48},{64,56},{72,6... | collective-permute-start | bytes 6152 | tf_op jit(solution)/shard_map/ppermute | solution.py:28
  37.3 9.3 %collective-permute-start.6 = (f32[2,258,1]{2,1,0:T(8,128)S(1)}, f32[2,258,1]{2,1,0:T(8,128)S(1)}, u32[]{:S(2)}, u32[]{:S(2)}) collective-permute-start(f32[2,258,1]{2,1,0:T(8,128)S(1)} %get-tuple-element.30), channel_id=1, source_target_pairs={{0,1},{1,2},{2,3},{3,4},{4,5},{5,6},{6,7},{7,128},{128,129},{129,1... | collective-permute-start | bytes 6200 | tf_op jit(solution)/shard_map/ppermute | solution.py:27
  41.8 10.4 %collective-permute-start.7 = (f32[2,258,1]{2,1,0:T(8,128)S(1)}, f32[2,258,1]{2,1,0:T(8,128)S(1)}, u32[]{:S(2)}, u32[]{:S(2)}) collective-permute-start(f32[2,258,1]{2,1,0:T(8,128)S(1)} %get-tuple-element.31), channel_id=1, source_target_pairs={{1,0},{2,1},{3,2},{4,3},{5,4},{6,5},{7,6},{128,7},{129,128},{130,1... | collective-permute-start | bytes 6200 | tf_op jit(solution)/shard_map/ppermute | solution.py:28
  53.8 28.2 %copy-start = (f32[2,256,256]{2,1,0:T(8,128)}, f32[2,256,256]{2,1,0:T(8,128)S(1)}, u32[]{:S(2)}) copy-start(f32[2,256,256]{2,1,0:T(8,128)S(1)} %get-tuple-element.10) | copy-start | bytes 1572868
  55.0 1.7 copy-start.9
  55.2 1.5 copy-start.11
  56.5 0.7 copy-start.19
  57.2 0.7 copy-start.20
  57.9 5.8 %collective-permute-start.8 = (f32[2,1,256]{2,1,0:T(1,128)S(1)}, f32[2,1,256]{2,1,0:T(1,128)S(1)}, u32[]{:S(2)}, u32[]{:S(2)}) collective-permute-start(f32[2,1,256]{2,1,0:T(1,128)S(1)} %get-tuple-element.68), channel_id=1, source_target_pairs={{0,8},{8,16},{16,24},{24,32},{32,40},{40,48},{48,56},{56,64},{64,7... | collective-permute-start | bytes 6152 | tf_op jit(solution)/shard_map/ppermute | solution.py:27
  59.8 7.6 %collective-permute-start.9 = (f32[2,1,256]{2,1,0:T(1,128)S(1)}, f32[2,1,256]{2,1,0:T(1,128)S(1)}, u32[]{:S(2)}, u32[]{:S(2)}) collective-permute-start(f32[2,1,256]{2,1,0:T(1,128)S(1)} %get-tuple-element.69), channel_id=1, source_target_pairs={{8,0},{16,8},{24,16},{32,24},{40,32},{48,40},{56,48},{64,56},{72,6... | collective-permute-start | bytes 6152 | tf_op jit(solution)/shard_map/ppermute | solution.py:28
  67.6 8.2 %collective-permute-start.10 = (f32[2,258,1]{2,1,0:T(8,128)S(1)}, f32[2,258,1]{2,1,0:T(8,128)S(1)}, u32[]{:S(2)}, u32[]{:S(2)}) collective-permute-start(f32[2,258,1]{2,1,0:T(8,128)S(1)} %get-tuple-element.28), channel_id=1, source_target_pairs={{0,1},{1,2},{2,3},{3,4},{4,5},{5,6},{6,7},{7,128},{128,129},{129,1... | collective-permute-start | bytes 6200 | tf_op jit(solution)/shard_map/ppermute | solution.py:27
  70.7 9.9 %collective-permute-start.11 = (f32[2,258,1]{2,1,0:T(8,128)S(1)}, f32[2,258,1]{2,1,0:T(8,128)S(1)}, u32[]{:S(2)}, u32[]{:S(2)}) collective-permute-start(f32[2,258,1]{2,1,0:T(8,128)S(1)} %get-tuple-element.29), channel_id=1, source_target_pairs={{1,0},{2,1},{3,2},{4,3},{5,4},{6,5},{7,6},{128,7},{129,128},{130,1... | collective-permute-start | bytes 6200 | tf_op jit(solution)/shard_map/ppermute | solution.py:28
  82.1 28.8 %copy-start.2 = (f32[2,256,256]{2,1,0:T(8,128)}, f32[2,256,256]{2,1,0:T(8,128)S(1)}, u32[]{:S(2)}) copy-start(f32[2,256,256]{2,1,0:T(8,128)S(1)} %get-tuple-element.8) | copy-start | bytes 1572868
  83.3 1.7 copy-start.13
  83.5 1.5 copy-start.14
  84.8 0.7 copy-start.21
  85.5 0.7 copy-start.22
  86.3 5.8 %collective-permute-start.12 = (f32[2,1,256]{2,1,0:T(1,128)S(1)}, f32[2,1,256]{2,1,0:T(1,128)S(1)}, u32[]{:S(2)}, u32[]{:S(2)}) collective-permute-start(f32[2,1,256]{2,1,0:T(1,128)S(1)} %get-tuple-element.50), channel_id=1, source_target_pairs={{0,8},{8,16},{16,24},{24,32},{32,40},{40,48},{48,56},{56,64},{64,7... | collective-permute-start | bytes 6152 | tf_op jit(solution)/shard_map/ppermute | solution.py:27
  88.2 7.6 %collective-permute-start.13 = (f32[2,1,256]{2,1,0:T(1,128)S(1)}, f32[2,1,256]{2,1,0:T(1,128)S(1)}, u32[]{:S(2)}, u32[]{:S(2)}) collective-permute-start(f32[2,1,256]{2,1,0:T(1,128)S(1)} %get-tuple-element.51), channel_id=1, source_target_pairs={{8,0},{16,8},{24,16},{32,24},{40,32},{48,40},{56,48},{64,56},{72,6... | collective-permute-start | bytes 6152 | tf_op jit(solution)/shard_map/ppermute | solution.py:28
  95.9 9.1 %collective-permute-start.14 = (f32[2,258,1]{2,1,0:T(8,128)S(1)}, f32[2,258,1]{2,1,0:T(8,128)S(1)}, u32[]{:S(2)}, u32[]{:S(2)}) collective-permute-start(f32[2,258,1]{2,1,0:T(8,128)S(1)} %get-tuple-element.26), channel_id=1, source_target_pairs={{0,1},{1,2},{2,3},{3,4},{4,5},{5,6},{6,7},{7,128},{128,129},{129,1... | collective-permute-start | bytes 6200 | tf_op jit(solution)/shard_map/ppermute | solution.py:27
  101.1 8.4 %collective-permute-start.15 = (f32[2,258,1]{2,1,0:T(8,128)S(1)}, f32[2,258,1]{2,1,0:T(8,128)S(1)}, u32[]{:S(2)}, u32[]{:S(2)}) collective-permute-start(f32[2,258,1]{2,1,0:T(8,128)S(1)} %get-tuple-element.27), channel_id=1, source_target_pairs={{1,0},{2,1},{3,2},{4,3},{5,4},{6,5},{7,6},{128,7},{129,128},{130,1... | collective-permute-start | bytes 6200 | tf_op jit(solution)/shard_map/ppermute | solution.py:28
  111.0 27.5 %copy-start.4 = (f32[2,256,256]{2,1,0:T(8,128)}, f32[2,256,256]{2,1,0:T(8,128)S(1)}, u32[]{:S(2)}) copy-start(f32[2,256,256]{2,1,0:T(8,128)S(1)} %get-tuple-element.6) | copy-start | bytes 1572868
  112.2 1.7 copy-start.15
  112.4 1.5 copy-start.16
  113.7 0.7 copy-start.23
  114.4 0.7 copy-start.24
  115.1 5.8 %collective-permute-start.16 = (f32[2,1,256]{2,1,0:T(1,128)S(1)}, f32[2,1,256]{2,1,0:T(1,128)S(1)}, u32[]{:S(2)}, u32[]{:S(2)}) collective-permute-start(f32[2,1,256]{2,1,0:T(1,128)S(1)} %get-tuple-element.32), channel_id=1, source_target_pairs={{0,8},{8,16},{16,24},{24,32},{32,40},{40,48},{48,56},{56,64},{64,7... | collective-permute-start | bytes 6152 | tf_op jit(solution)/shard_map/ppermute | solution.py:27
  117.1 7.6 %collective-permute-start.17 = (f32[2,1,256]{2,1,0:T(1,128)S(1)}, f32[2,1,256]{2,1,0:T(1,128)S(1)}, u32[]{:S(2)}, u32[]{:S(2)}) collective-permute-start(f32[2,1,256]{2,1,0:T(1,128)S(1)} %get-tuple-element.33), channel_id=1, source_target_pairs={{8,0},{16,8},{24,16},{32,24},{40,32},{48,40},{56,48},{64,56},{72,6... | collective-permute-start | bytes 6152 | tf_op jit(solution)/shard_map/ppermute | solution.py:28
  124.8 7.9 %collective-permute-start.18 = (f32[2,258,1]{2,1,0:T(8,128)S(1)}, f32[2,258,1]{2,1,0:T(8,128)S(1)}, u32[]{:S(2)}, u32[]{:S(2)}) collective-permute-start(f32[2,258,1]{2,1,0:T(8,128)S(1)} %get-tuple-element.24), channel_id=1, source_target_pairs={{0,1},{1,2},{2,3},{3,4},{4,5},{5,6},{6,7},{7,128},{128,129},{129,1... | collective-permute-start | bytes 6200 | tf_op jit(solution)/shard_map/ppermute | solution.py:27
  128.8 8.4 %collective-permute-start.19 = (f32[2,258,1]{2,1,0:T(8,128)S(1)}, f32[2,258,1]{2,1,0:T(8,128)S(1)}, u32[]{:S(2)}, u32[]{:S(2)}) collective-permute-start(f32[2,258,1]{2,1,0:T(8,128)S(1)} %get-tuple-element.25), channel_id=1, source_target_pairs={{1,0},{2,1},{3,2},{4,3},{5,4},{6,5},{7,6},{128,7},{129,128},{130,1... | collective-permute-start | bytes 6200 | tf_op jit(solution)/shard_map/ppermute | solution.py:28
  139.4 42.1 %copy-start.1 = (f32[2,256,256]{2,1,0:T(8,128)S(1)}, f32[2,256,256]{2,1,0:T(8,128)}, u32[]{:S(2)}) copy-start(f32[2,256,256]{2,1,0:T(8,128)} %copy-done) | copy-start | bytes 1572868
  139.4 42.1 %copy-start.3 = (f32[2,256,256]{2,1,0:T(8,128)S(1)}, f32[2,256,256]{2,1,0:T(8,128)}, u32[]{:S(2)}) copy-start(f32[2,256,256]{2,1,0:T(8,128)} %copy-done.2) | copy-start | bytes 1572868
  139.5 42.1 %copy-start.5 = (f32[2,256,256]{2,1,0:T(8,128)S(1)}, f32[2,256,256]{2,1,0:T(8,128)}, u32[]{:S(2)}) copy-start(f32[2,256,256]{2,1,0:T(8,128)} %copy-done.4) | copy-start | bytes 1572868
  139.5 42.1 %copy-start.7 = (f32[2,256,256]{2,1,0:T(8,128)S(1)}, f32[2,256,256]{2,1,0:T(8,128)}, u32[]{:S(2)}) copy-start(f32[2,256,256]{2,1,0:T(8,128)} %copy-done.6) | copy-start | bytes 1572868
  139.5 42.1 %copy-start.10 = (f32[1,256,256]{2,1,0:T(8,128)S(1)}, f32[1,256,256]{2,1,0:T(8,128)}, u32[]{:S(2)}) copy-start(f32[1,256,256]{2,1,0:T(8,128)} %copy-done.9) | copy-start | bytes 786436
  139.5 42.1 %copy-start.12 = (f32[1,256,256]{2,1,0:T(8,128)S(1)}, f32[1,256,256]{2,1,0:T(8,128)}, u32[]{:S(2)}) copy-start(f32[1,256,256]{2,1,0:T(8,128)} %copy-done.11) | copy-start | bytes 786436
  142.6 1.4 collective-permute-start.20
  144.7 3.6 %collective-permute-start.21 = (f32[8,128]{1,0:T(8,128)S(1)}, f32[8,128]{1,0:T(8,128)S(1)}, u32[]{:S(2)}, u32[]{:S(2)}) collective-permute-start(f32[8,128]{1,0:T(8,128)S(1)} %add.734), channel_id=1, source_target_pairs={{0,8},{8,0},{16,24},{24,16},{32,40},{40,32},{48,56},{56,48},{64,72... | collective-permute-start | bytes 12296 | tf_op jit(solution)/shard_map/ppermute | solution.py:254
  148.3 5.1 %collective-permute-start.22 = (f32[8,128]{1,0:T(8,128)S(1)}, f32[8,128]{1,0:T(8,128)S(1)}, u32[]{:S(2)}, u32[]{:S(2)}) collective-permute-start(f32[8,128]{1,0:T(8,128)S(1)} %add.735), channel_id=1, source_target_pairs={{0,16},{8,24},{16,0},{24,8},{32,48},{40,56},{48,32},{56,40},{64,80... | collective-permute-start | bytes 12296 | tf_op jit(solution)/shard_map/ppermute | solution.py:254
  153.4 3.6 %collective-permute-start.23 = (f32[8,128]{1,0:T(8,128)S(1)}, f32[8,128]{1,0:T(8,128)S(1)}, u32[]{:S(2)}, u32[]{:S(2)}) collective-permute-start(f32[8,128]{1,0:T(8,128)S(1)} %add.736), channel_id=1, source_target_pairs={{0,32},{8,40},{16,48},{24,56},{32,0},{40,8},{48,16},{56,24},{64,96... | collective-permute-start | bytes 12296 | tf_op jit(solution)/shard_map/ppermute | solution.py:254
  157.0 5.1 %collective-permute-start.24 = (f32[8,128]{1,0:T(8,128)S(1)}, f32[8,128]{1,0:T(8,128)S(1)}, u32[]{:S(2)}, u32[]{:S(2)}) collective-permute-start(f32[8,128]{1,0:T(8,128)S(1)} %add.737), channel_id=1, source_target_pairs={{0,64},{8,72},{16,80},{24,88},{32,96},{40,104},{48,112},{56,120},{... | collective-permute-start | bytes 12296 | tf_op jit(solution)/shard_map/ppermute | solution.py:254
  162.1 3.6 %collective-permute-start.25 = (f32[8,128]{1,0:T(8,128)S(1)}, f32[8,128]{1,0:T(8,128)S(1)}, u32[]{:S(2)}, u32[]{:S(2)}) collective-permute-start(f32[8,128]{1,0:T(8,128)S(1)} %add.738), channel_id=1, source_target_pairs={{0,1},{1,0},{2,3},{3,2},{4,5},{5,4},{6,7},{7,6},{8,9},{9,8},{10,11... | collective-permute-start | bytes 12296 | tf_op jit(solution)/shard_map/ppermute | solution.py:254
  165.7 4.5 %collective-permute-start.26 = (f32[8,128]{1,0:T(8,128)S(1)}, f32[8,128]{1,0:T(8,128)S(1)}, u32[]{:S(2)}, u32[]{:S(2)}) collective-permute-start(f32[8,128]{1,0:T(8,128)S(1)} %add.739), channel_id=1, source_target_pairs={{0,2},{1,3},{2,0},{3,1},{4,6},{5,7},{6,4},{7,5},{8,10},{9,11},{10,... | collective-permute-start | bytes 12296 | tf_op jit(solution)/shard_map/ppermute | solution.py:254
  170.2 7.5 %collective-permute-start.27 = (f32[8,128]{1,0:T(8,128)S(1)}, f32[8,128]{1,0:T(8,128)S(1)}, u32[]{:S(2)}, u32[]{:S(2)}) collective-permute-start(f32[8,128]{1,0:T(8,128)S(1)} %add.740), channel_id=1, source_target_pairs={{0,4},{1,5},{2,6},{3,7},{4,0},{5,1},{6,2},{7,3},{8,12},{9,13},{10,... | collective-permute-start | bytes 12296 | tf_op jit(solution)/shard_map/ppermute | solution.py:254
